TPU v7x, 128 devices: a whole 4x4x4 slice. The times are simulated.
128 devices in a mesh: req: 32 (over y, z_lo, x), exp: 4 (over z_hi, core).
Axes of the slice: x: 4, y: 4, z: 4 (z_hi: 2, z_lo: 2; z = z_hi * 2 + z_lo), core: 2. Of those that a mesh axis runs over, the one named last changes fastest.
Arguments:
- activations: bfloat16 [16384, 1536], P('req'), may hold values from -6 to 6
- attn_gain: float32 [1536], replicated, may hold values from 0.1 to 1.9
- w_query: bfloat16 [1536, 1536], P(None, 'exp'), may hold values from -0.15625 to 0.15625
- key_value_weight: bfloat16 [1536, 2, 256], replicated, may hold values from -0.15625 to 0.15625
- w_output: bfloat16 [1536, 1536], P('exp'), may hold values from -0.15625 to 0.15625
- group_prefix_cache: bfloat16 [8192, 2, 2, 128], P('req')
- lengths: int32 [64], replicated, may hold values from 64 to 448, as said below
- groups: int32 [64], replicated, may hold values from 0 to 3
- owners: int32 [32], replicated, may hold values from 0 to 31, each once
- moe_gain: float32 [1536], replicated, may hold values from 0.1 to 1.9
- w_gate: bfloat16 [32, 1536, 768], P('req', None, 'exp'), may hold values from -0.15625 to 0.15625
- w_up: bfloat16 [32, 1536, 768], P('req', None, 'exp'), may hold values from -0.15625 to 0.15625
- w_down: bfloat16 [32, 768, 1536], P('req', 'exp'), may hold values from -0.21875 to 0.21875
- picks: int32 [16384, 4], P('req'), may hold values from 0 to 31, all different within a row; in each aligned block of 512 rows (0 to 511, 512 to 1023, ...) at most 128 rows name the same one
- pick_weight: float32 [16384, 4], P('req'), may hold values from 0.05 to 0.6
Outputs:
- out: bfloat16 [16384, 1536], P('req')
Inputs may be any that keep to these rules, and one draw needn't show every extreme that they name: `lengths`: entries 2r and 2r+1 sum to 512; every entry is a multiple of 64. `owners`: each value appears once. `picks`: a row names 4 different experts; in the rows of one index of req no expert is named by more than 128 rows.
All inputs are finite; a program needn't handle non-finite values.
Results may differ from a plain program's by a relative error of at most 0.0073.
Values may be sent and summed in bfloat16 or wider, within the bound.
No kernel may reach another device: no remote copies, remote signals or barrier semaphores. Data moves between devices by JAX's collectives and lax.ppermute only.
A program may use at most 128 MiB of HBM per device.

v0:
```python
import jax
import jax.numpy as jnp
from jax import lax
from jax.sharding import PartitionSpec as P

QUERY_HEADS = 12
KEY_VALUE_HEADS = 2
HEAD_SIZE = 128
TOP = 4
GROUPS = 4
REQ_DEV = 2
LMIN = 64


EPS = 1e-06


def rms_scale(rows, gain):
    rows32 = rows.astype(jnp.float32)
    inverse = lax.rsqrt(jnp.mean(rows32 * rows32, axis=-1, keepdims=True) + EPS)
    return (rows32 * inverse * gain).astype(jnp.bfloat16)


def prefix_for(gathered, owners, group, per_group):
    prefix_segments = lax.dynamic_slice_in_dim(owners, group * per_group, per_group, 0)
    return gathered[prefix_segments].reshape(per_group * gathered.shape[1], 2, gathered.shape[3])


def req_shift_pairs(n_req, kind, d):
    pairs = []
    for r in range(n_req):
        if kind == "x":
            dest = (r // 4) * 4 + (r % 4 + d) % 4
        elif kind == "z":
            dest = r ^ 4
        else:
            dest = (r + 8 * d) % n_req
        pairs.append((r, dest))
    return pairs


def exp_flip(x, n_exp, bit):
    return lax.ppermute(x, "exp", [(e, e ^ bit) for e in range(n_exp)])


def gather_exp(x, axis, n_exp):
    far = exp_flip(x, n_exp, 2)
    near = exp_flip(jnp.concatenate([x, far], axis=axis), n_exp, 1)
    return jnp.concatenate([x, far, near], axis=axis)


def far_relay(x, n_req, n_exp):
    def index(r, e):
        return r * n_exp + e

    first = []
    second = []
    for r in range(n_req):
        for e in range(n_exp):
            if e % 2 == 0:
                first.append((index(r, e), index(r ^ 4, e)))
                second.append((index(r, e), index(r ^ 4, e ^ 2)))
            else:
                first.append((index(r, e), index(r ^ 4, e ^ 2)))
                second.append((index(r, e), index(r ^ 4, e)))
    hop = lax.ppermute(x, ("req", "exp"), first)
    return lax.ppermute(hop, ("req", "exp"), second)


def gather_exp_relay(x, axis, n_req, n_exp):
    far = far_relay(x, n_req, n_exp)
    near = exp_flip(jnp.concatenate([x, far], axis=axis), n_exp, 1)
    return jnp.concatenate([x, far, near], axis=axis)


def gather_prefix_near(mine, n_req):
    return jnp.stack([mine, lax.ppermute(mine, "req", req_shift_pairs(n_req, "z", 1))])


def gather_prefix_halves(along_z, n_req):
    along_x = jnp.stack(
        [along_z] + [lax.ppermute(along_z, "req", req_shift_pairs(n_req, "x", d)) for d in (1, 2, 3)]
    )
    along_y = jnp.stack(
        [along_x] + [lax.ppermute(along_x, "req", req_shift_pairs(n_req, "y", d)) for d in (1, 2, 3)]
    )
    return along_y.reshape((n_req,) + along_z.shape[1:])


def body(
    activations,
    attn_gain,
    w_query,
    key_value_weight,
    w_output,
    group_prefix_cache,
    lengths,
    groups,
    owners,
    moe_gain,
    w_gate,
    w_up,
    w_down,
    picks,
    pick_weight,
):
    req_index = lax.axis_index("req")
    expert_index = lax.axis_index("exp")
    n_req = lax.axis_size("req")
    n_exp = lax.axis_size("exp")
    tok = activations.shape[0]
    width_model = activations.shape[1]
    heads_per_shard = w_query.shape[1] // HEAD_SIZE
    key_value_head = expert_index * heads_per_shard // (QUERY_HEADS // KEY_VALUE_HEADS)

    own_piece = lax.dynamic_index_in_dim(group_prefix_cache, key_value_head, 2, keepdims=False)
    core = expert_index % 2
    far_half = expert_index // 2
    half_rows = own_piece.shape[0] // 2
    mine = lax.dynamic_slice_in_dim(own_piece, core * half_rows, half_rows, 0)
    along_z = gather_prefix_near(mine, n_req)
    ff_shard = w_gate.shape[2]
    packed = jnp.concatenate([w_gate[0].T, w_up[0].T, w_down[0]], axis=0)
    w_output_late, packed_late, along_z = lax.optimization_barrier((w_output, packed, along_z))
    halves_mine = gather_prefix_halves(along_z, n_req)
    halves_other = exp_flip(halves_mine, n_exp, 1)
    w_output_full = gather_exp_relay(w_output_late, 0, n_req, n_exp)
    packed_full = gather_exp_relay(packed_late.reshape(1, 3 * ff_shard, -1), 0, n_req, n_exp)
    gate_full = packed_full[:, :ff_shard].reshape(-1, packed.shape[1]).T
    up_full = packed_full[:, ff_shard : 2 * ff_shard].reshape(-1, packed.shape[1]).T
    down_full = packed_full[:, 2 * ff_shard :].reshape(-1, packed.shape[1])

    normalized_input = rms_scale(activations, attn_gain)
    query_rows = (
        jnp.dot(normalized_input, w_query, preferred_element_type=jnp.float32) * HEAD_SIZE ** (-0.5)
    ).astype(jnp.bfloat16)
    query_rows = query_rows.reshape(tok, heads_per_shard, HEAD_SIZE)
    kv_weight = lax.dynamic_slice_in_dim(key_value_weight, key_value_head * HEAD_SIZE, HEAD_SIZE, 2)
    local_key_value = jnp.einsum(
        "td,dcf->tcf", normalized_input, kv_weight, preferred_element_type=jnp.float32
    ).astype(jnp.bfloat16)

    pair = lax.dynamic_slice_in_dim(lengths, req_index * REQ_DEV, REQ_DEV, 0)
    pair_groups = lax.dynamic_slice_in_dim(groups, req_index * REQ_DEV, REQ_DEV, 0)
    per_group = n_req // GROUPS
    positions = jnp.arange(tok)
    in_first = positions < pair[0]
    my_y, my_z, my_x = req_index // 8, (req_index // 4) % 2, req_index % 4

    def prefix_of(group):
        owner = lax.dynamic_slice_in_dim(owners, group * per_group, per_group, 0)
        where = ((my_y - owner // 8) % 4) * 8 + ((my_x - owner % 4) % 4) * 2 + (my_z - (owner // 4) % 2) % 2
        part_mine = halves_mine[where]
        part_other = halves_other[where]
        rows = jnp.concatenate([part_mine, part_other], axis=1)
        return rows.reshape(per_group * 2 * half_rows, 2, HEAD_SIZE)

    prefix_a = prefix_of(pair_groups[0])
    prefix_b = prefix_of(pair_groups[1])
    zero_q = jnp.zeros_like(query_rows)
    first3 = in_first[:, None, None]
    query_ab = jnp.concatenate(
        [jnp.where(first3, query_rows, zero_q), jnp.where(first3, zero_q, query_rows)], axis=-1
    )
    keys_ab = jnp.concatenate([prefix_a[:, 0], prefix_b[:, 0]], axis=-1)
    values_ab = jnp.concatenate([prefix_a[:, 1], prefix_b[:, 1]], axis=-1)
    pre_scores = jnp.einsum("thd,pd->htp", query_ab, keys_ab, preferred_element_type=jnp.float32)
    suf_scores = jnp.einsum(
        "thd,sd->hts", query_rows, local_key_value[:, 0], preferred_element_type=jnp.float32
    )
    allowed = (positions[None, :] <= positions[:, None]) & (in_first[:, None] == in_first[None, :])
    suf_scores = jnp.where(allowed[None], suf_scores, -jnp.inf)
    top = jnp.maximum(
        jnp.max(pre_scores, axis=-1, keepdims=True), jnp.max(suf_scores, axis=-1, keepdims=True)
    )
    pre_exp = jnp.exp(pre_scores - top)
    suf_exp = jnp.exp(suf_scores - top)
    denom = jnp.sum(pre_exp, axis=-1, keepdims=True) + jnp.sum(suf_exp, axis=-1, keepdims=True)
    pre_w = (pre_exp / denom).astype(jnp.bfloat16)
    suf_w = (suf_exp / denom).astype(jnp.bfloat16)
    pre_ctx_ab = jnp.einsum("htp,pd->thd", pre_w, values_ab, preferred_element_type=jnp.float32)
    pre_ctx = jnp.where(first3, pre_ctx_ab[..., :HEAD_SIZE], pre_ctx_ab[..., HEAD_SIZE:])
    suf_ctx = jnp.einsum(
        "hts,sd->thd", suf_w, local_key_value[:, 1], preferred_element_type=jnp.float32
    )
    context = (pre_ctx + suf_ctx).astype(jnp.bfloat16)
    context = context.reshape(tok, heads_per_shard * HEAD_SIZE)
    context_full = gather_exp(context, 1, n_exp)
    attn = jnp.dot(context_full, w_output_full, preferred_element_type=jnp.float32)
    resid = (activations.astype(jnp.float32) + attn).astype(jnp.bfloat16)
    normed_moe = rms_scale(resid, moe_gain)

    n_experts = n_req
    cap = min(tok, 2 * tok * TOP // n_req)
    quarter = cap // n_exp
    expert_ids = jnp.arange(n_experts, dtype=jnp.int32)
    chose = jnp.any(picks[:, :, None] == expert_ids[None, None, :], axis=1).astype(jnp.bfloat16)
    earlier = (positions[None, :] < positions[:, None]).astype(jnp.bfloat16)
    before = jnp.dot(earlier, chose, preferred_element_type=jnp.float32).astype(jnp.int32)
    pick_hot = picks[:, :, None] == expert_ids[None, None, :]
    slot = jnp.sum(jnp.where(pick_hot, before[:, None, :], 0), axis=2)
    local = slot - expert_index * quarter
    keep = (local >= 0) & (local < quarter)
    target = jnp.where(keep, picks * quarter + local, -1)
    columns = jnp.arange(n_experts * quarter, dtype=jnp.int32)
    hits = target[:, :, None] == columns[None, None, :]
    dispatch = jnp.any(hits, axis=1).astype(jnp.bfloat16)
    send = jnp.einsum("tq,td->qd", dispatch, normed_moe, preferred_element_type=jnp.float32)
    send = send.astype(jnp.bfloat16).reshape(n_experts, quarter, width_model)
    received = lax.all_to_all(send, "req", split_axis=0, concat_axis=0, tiled=True)
    rows = received.reshape(-1, width_model)
    gate = jnp.dot(rows, gate_full, preferred_element_type=jnp.float32)
    up = jnp.dot(rows, up_full, preferred_element_type=jnp.float32)
    hidden = (jnp.maximum(gate, 0.0) * up).astype(jnp.bfloat16)
    part = jnp.dot(hidden, down_full, preferred_element_type=jnp.float32).astype(jnp.bfloat16)
    part = part.reshape(n_experts, quarter, width_model)
    back = lax.all_to_all(part, "req", split_axis=0, concat_axis=0, tiled=True)
    back = back.reshape(-1, width_model)
    combine = jnp.sum(jnp.where(hits, pick_weight[:, :, None], 0.0), axis=1)
    half_tok = tok // 2
    quarter_tok = tok // 4

    def mix_rows(first_row, count):
        weights = lax.dynamic_slice_in_dim(combine, first_row, count, 0)
        weights_hi = weights.astype(jnp.bfloat16)
        weights_lo = (weights - weights_hi.astype(jnp.float32)).astype(jnp.bfloat16)
        return jnp.dot(weights_hi, back, preferred_element_type=jnp.float32) + jnp.dot(
            weights_lo, back, preferred_element_type=jnp.float32
        )

    give_half = mix_rows((1 - core) * half_tok, half_tok)
    got_half = exp_flip(give_half, n_exp, 1)
    my_half = core * half_tok
    give_q = mix_rows(my_half + (1 - far_half) * quarter_tok, quarter_tok) + lax.dynamic_slice_in_dim(
        got_half, (1 - far_half) * quarter_tok, quarter_tok, 0
    )
    got_q = exp_flip(give_q, n_exp, 2)
    my_rows = my_half + far_half * quarter_tok
    keep_q = mix_rows(my_rows, quarter_tok) + lax.dynamic_slice_in_dim(
        got_half, far_half * quarter_tok, quarter_tok, 0
    )
    quarter_sum = keep_q + got_q
    resid_rows = lax.dynamic_slice_in_dim(resid, my_rows, quarter_tok, 0)
    out_q = (resid_rows.astype(jnp.float32) + quarter_sum).astype(jnp.bfloat16)
    other_q = exp_flip(out_q, n_exp, 2)
    out_half = jnp.zeros((half_tok, width_model), jnp.bfloat16)
    out_half = lax.dynamic_update_slice_in_dim(out_half, out_q, far_half * quarter_tok, 0)
    out_half = lax.dynamic_update_slice_in_dim(out_half, other_q, (1 - far_half) * quarter_tok, 0)
    other_half = exp_flip(out_half, n_exp, 1)
    out = jnp.zeros((tok, width_model), jnp.bfloat16)
    out = lax.dynamic_update_slice_in_dim(out, out_half, my_half, 0)
    return lax.dynamic_update_slice_in_dim(out, other_half, (1 - core) * half_tok, 0)


def solution(mesh):
    return jax.shard_map(
        body,
        mesh=mesh,
        in_specs=(
            P("req", None),
            P(),
            P(None, "exp"),
            P(),
            P("exp", None),
            P("req", None, None, None),
            P(),
            P(),
            P(),
            P(),
            P("req", None, "exp"),
            P("req", None, "exp"),
            P("req", "exp", None),
            P("req", None),
            P("req", None),
        ),
        out_specs=P("req", None),
        check_vma=False,
    )
```

profile of v0, /device:TPU:3, one launch (start us, length us, event | category | flops | bytes accessed | tf_op | source)
XLA Modules:
  0.0 286.7 jit_solution(7123539907057598512)
XLA Ops:
  8.7 2.7 collective-permute-done.2
  15.8 2.6 collective-permute-start.5
  19.9 3.5 %collective-permute-start.10 = (bf16[384,1536]{1,0:T(8,128)(2,1)}, bf16[384,1536]{1,0:T(8,128)(2,1)}, u32[]{:S(2)}, u32[]{:S(2)}) collective-permute-start(bf16[384,1536]{1,0:T(8,128)(2,1)} %param.19), channel_id=1, source_target_pairs={{0,16},{1,19},{2,18},{3,17},{4,20},{5,23},{6,22},{7,21},{8,24},{9,... | collective-permute-start | bytes 3538952 | tf_op jit(solution)/shard_map/ppermute | solution.py:66
  26.7 12.3 %collective-permute-done.5 = bf16[4,2,128,2,128]{4,2,3,1,0:T(8,128)(2,1)} collective-permute-done((bf16[4,2,128,2,128]{4,2,3,1,0:T(8,128)(2,1)}, bf16[4,2,128,2,128]{4,2,3,1,0:T(8,128)(2,1)}, u32[]{:S(2)}, u32[]{:S(2)}) %collective-permute-start.5) | collective-permute-done | bytes 524320 | tf_op jit(solution)/shard_map/ppermute | solution.py:85
  40.8 3.1 %pad_maximum_fusion.3 = bf16[4,4,2,128,2,128]{5,3,4,2,1,0:T(8,128)(2,1)} fusion(bf16[1,4,2,128,2,128]{5,3,4,2,1,0:T(8,128)(2,1)} %bitcast.16, bf16[1,4,2,128,2,128]{5,3,4,2,1,0:T(8,128)(2,1)} %bitcast.15, bf16[1,4,2,128,2,128]{5,3,4,2,1,0:T(8,128)(2,1)} %bitcast.14, bf16[1,4,2,128,2,128]{5,3,4,2,1,0:T(8,128)(2,1)} %get-tuple-element.20), kind=kLoop, calls=%fused_computation.45 | loop fusion | flops 3145728 | bytes 4194304 | tf_op jit(solution)/shard_map/stack | solution.py:84
  55.2 2.2 fusion.19
  62.1 9.5 %collective-permute-done.11 = bf16[384,1536]{1,0:T(8,128)(2,1)} collective-permute-done((bf16[384,1536]{1,0:T(8,128)(2,1)}, bf16[384,1536]{1,0:T(8,128)(2,1)}, u32[]{:S(2)}, u32[]{:S(2)}) %collective-permute-start.11) | collective-permute-done | bytes 1179680 | tf_op jit(solution)/shard_map/ppermute | solution.py:67
  71.6 3.2 %pad_maximum_fusion.2 = bf16[768,1536]{1,0:T(8,128)(2,1)} fusion(bf16[384,1536]{1,0:T(8,128)(2,1)} %collective-permute-done.11, bf16[384,1536]{1,0:T(8,128)(2,1)} %param.19), kind=kLoop, calls=%fused_computation.44 | loop fusion | flops 4718592 | bytes 4718592 | tf_op jit(solution)/shard_map/concatenate | solution.py:72
  74.8 3.0 %gather_fusion.1 = bf16[8,128,2,128]{3,1,2,0:T(8,128)(2,1)} fusion(bf16[32,128,2,128]{3,1,2,0:T(8,128)(2,1)} %collective-permute-done.7, s32[1024]{0:T(1024)S(1)} %get-tuple-element.37), kind=kCustom, calls=%fused_computation.1 | custom fusion | bytes 1048608 | tf_op jit(solution)/shard_map/gather | solution.py:154
  79.9 3.0 %gather_fusion.3 = bf16[8,128,2,128]{3,1,2,0:T(8,128)(2,1)} fusion(bf16[32,128,2,128]{3,1,2,0:T(8,128)(2,1)} %collective-permute-done.7, s32[1024]{0:T(1024)S(1)} %get-tuple-element.36), kind=kCustom, calls=%fused_computation.3 | custom fusion | bytes 1048608 | tf_op jit(solution)/shard_map/gather | solution.py:154
  89.5 3.5 %fusion.32 = f32[512,3,256]{2,0,1:T(8,128)S(1)} fusion(f32[2048,512,3]{1,0,2:T(8,128)S(1)} %get-tuple-element.31, f32[3,512]{1,0:T(4,128)S(1)} %add.212, f32[3,512]{1,0:T(4,128)S(1)} %max.14, bf16[2048,128]{1,0:T(8,128)(2,1)S(1)} %copy-done.13, bf16[2048,128]{1,0:T(8,128)(2,1)S(1)} %copy-done.12), kind=kOutput, calls=%fused_computation.57 | convolution fusion | flops 1622147072 | bytes 15216640 | tf_op jit(solution)/shard_map/htp,pd->thd/dot_general | solution.py:181
  94.3 3.5 %collective-permute-start.8 = (bf16[512,384]{0,1:T(8,128)(2,1)S(1)}, bf16[512,384]{0,1:T(8,128)(2,1)S(1)}, u32[]{:S(2)}, u32[]{:S(2)}) collective-permute-start(bf16[512,384]{0,1:T(8,128)(2,1)S(1)} %bitcast.139), channel_id=1, source_target_pairs={{0,2},{1,3},{2,0},{3,1},{4,6},{5,7},{6,4},{7,5},{8,10},{9,11},{10,... | collective-permute-start | bytes 1179656 | tf_op jit(solution)/shard_map/ppermute | solution.py:43
  98.1 8.7 %collective-permute-done.8 = bf16[512,384]{0,1:T(8,128)(2,1)S(1)} collective-permute-done((bf16[512,384]{0,1:T(8,128)(2,1)S(1)}, bf16[512,384]{0,1:T(8,128)(2,1)S(1)}, u32[]{:S(2)}, u32[]{:S(2)}) %collective-permute-start.8) | collective-permute-done | bytes 393248 | tf_op jit(solution)/shard_map/ppermute | solution.py:43
  108.1 3.7 %pad_maximum_fusion.1 = bf16[2,576,1536]{2,1,0:T(8,128)(2,1)} fusion(bf16[1,576,1536]{2,1,0:T(8,128)(2,1)} %collective-permute-done.14, bf16[1,576,1536]{2,1,0:T(8,128)(2,1)S(1)} %bitcast.130), kind=kLoop, calls=%fused_computation.27 | loop fusion | flops 1769472 | bytes 7077888 | tf_op jit(solution)/shard_map/concatenate | solution.py:72
  113.5 5.5 %fusion.10 = (f32[512]{0:T(512)S(1)}, bf16[512,1536]{1,0:T(8,128)(2,1)S(1)}) fusion(bf16[768,1536]{1,0:T(8,128)(2,1)} %collective-permute-done.12, bf16[384,1536]{1,0:T(8,128)(2,1)} %collective-permute-done.11, bf16[384,1536]{1,0:T(8,128)(2,1)} %param.19, bf16[512,768]{0,1:T(8,128)(2,1)} %collective-permute-done.9, ...), kind=kOutput, calls=%fused_computation.28 | convolution fusion | flops 2439511552 | bytes 9439232 | tf_op jit(solution)/shard_map/dot_general | solution.py:189
  119.1 3.8 %convolution_convert_fusion.1 = bf16[1024,1536]{1,0:T(8,128)(2,1)} fusion(pred[512,1024]{1,0:T(8,128)(4,1)S(1)} %fusion.2, bf16[512,1536]{1,0:T(8,128)(2,1)S(1)} %get-tuple-element.35, f32[1536]{0:T(1024)S(1)} %copy-done.20, f32[512]{0:T(512)S(1)} %add_rsqrt_fusion), kind=kOutput, calls=%fused_computation.26 | convolution fusion | flops 1615331328 | bytes 5251072 | tf_op jit(solution)/shard_map/tq,td->qd/dot_general | solution.py:208
  122.8 5.1 %all-to-all-start = ((bf16[32,32,1536]{2,1,0:T(8,128)(2,1)}), bf16[32,32,1536]{2,1,0:T(8,128)(2,1)}, u32[]{:S(2)}, u32[]{:S(2)}) async-start(bf16[32,32,1536]{2,1,0:T(8,128)(2,1)} %bitcast.134), calls=%async_computation | async-start | bytes 6291456 | tf_op jit(solution)/shard_map/all_to_all | solution.py:210
  128.0 3.4 %pad_maximum_fusion = bf16[4,576,1536]{2,1,0:T(8,128)(2,1)S(1)} fusion(bf16[2,576,1536]{2,1,0:T(8,128)(2,1)} %collective-permute-done.15, bf16[1,576,1536]{2,1,0:T(8,128)(2,1)} %collective-permute-done.14, bf16[1,576,1536]{2,1,0:T(8,128)(2,1)S(1)} %bitcast.131), kind=kLoop, calls=%fused_computation.12 | loop fusion | flops 7077888 | bytes 14155776 | tf_op jit(solution)/shard_map/concatenate | solution.py:73
  131.4 2.6 fusion.89
  134.1 36.2 %all-to-all-done = bf16[32,32,1536]{2,1,0:T(8,128)(2,1)} async-done(((bf16[32,32,1536]{2,1,0:T(8,128)(2,1)}), bf16[32,32,1536]{2,1,0:T(8,128)(2,1)}, u32[]{:S(2)}, u32[]{:S(2)}) %all-to-all-start) | async-done | bytes 3145760 | tf_op jit(solution)/shard_map/all_to_all | solution.py:210
  170.3 6.9 %fusion.91 = f32[1024,768]{1,0:T(8,128)} fusion(bf16[1024,1536]{1,0:T(8,128)(2,1)} %bitcast.40, bf16[768,1536]{1,0:T(8,128)(2,1)} %bitcast.138), kind=kOutput, calls=%fused_computation.198 | convolution fusion | flops 2415919104 | bytes 8650752 | tf_op jit(solution)/shard_map/dot_general | solution.py:212
  177.2 10.2 %convolution_convert_fusion = bf16[1024,1536]{1,0:T(8,128)(2,1)} fusion(bf16[768,1536]{1,0:T(8,128)(2,1)} %bitcast.137, f32[1024,768]{1,0:T(8,128)} %fusion.91, bf16[1024,1536]{1,0:T(8,128)(2,1)} %bitcast.40, bf16[768,1536]{1,0:T(8,128)(2,1)S(1)} %bitcast.136), kind=kOutput, calls=%fused_computation.25 | convolution fusion | flops 4835770368 | bytes 14155776 | tf_op jit(solution)/shard_map/dot_general | solution.py:215
  187.3 5.0 %all-to-all-start.1 = ((bf16[32,32,1536]{2,1,0:T(8,128)(2,1)}), bf16[32,32,1536]{2,1,0:T(8,128)(2,1)S(1)}, u32[]{:S(2)}, u32[]{:S(2)}) async-start(bf16[32,32,1536]{2,1,0:T(8,128)(2,1)} %bitcast.135), calls=%async_computation.1 | async-start | bytes 6291456 | tf_op jit(solution)/shard_map/all_to_all | solution.py:217
  192.4 2.7 select_reduce_fusion
  195.0 39.6 %all-to-all-done.1 = bf16[32,32,1536]{2,1,0:T(8,128)(2,1)S(1)} async-done(((bf16[32,32,1536]{2,1,0:T(8,128)(2,1)}), bf16[32,32,1536]{2,1,0:T(8,128)(2,1)S(1)}, u32[]{:S(2)}, u32[]{:S(2)}) %all-to-all-start.1) | async-done | bytes 3145760 | tf_op jit(solution)/shard_map/all_to_all | solution.py:217
  234.7 2.3 fusion.53
  239.2 2.3 collective-permute-start.16
  244.9 2.8 dynamic-slice_add_fusion
  247.7 3.3 %collective-permute-start.17 = (f32[128,1536]{1,0:T(8,128)}, f32[128,1536]{1,0:T(8,128)}, u32[]{:S(2)}, u32[]{:S(2)}) collective-permute-start(f32[128,1536]{1,0:T(8,128)} %dynamic-slice_add_fusion), channel_id=1, source_target_pairs={{0,2},{1,3},{2,0},{3,1},{4,6},{5,7},{6,4},{7,5},{8,10},{9,11},{10,... | collective-permute-start | bytes 2359304 | tf_op jit(solution)/shard_map/ppermute | solution.py:43
  254.3 14.6 %collective-permute-done.17 = f32[128,1536]{1,0:T(8,128)} collective-permute-done((f32[128,1536]{1,0:T(8,128)}, f32[128,1536]{1,0:T(8,128)}, u32[]{:S(2)}, u32[]{:S(2)}) %collective-permute-start.17) | collective-permute-done | bytes 786464 | tf_op jit(solution)/shard_map/ppermute | solution.py:43
  270.7 2.8 collective-permute-start.18
  273.4 8.5 %collective-permute-done.18 = bf16[128,1536]{1,0:T(8,128)(2,1)S(1)} collective-permute-done((bf16[128,1536]{1,0:T(8,128)(2,1)S(1)}, bf16[128,1536]{1,0:T(8,128)(2,1)S(1)}, u32[]{:S(2)}, u32[]{:S(2)}) %collective-permute-start.18) | collective-permute-done | bytes 393248 | tf_op jit(solution)/shard_map/ppermute | solution.py:43
  (125 shorter events, 62.6 us)
Async XLA Ops:
  0.0 49.8 %copy-start = (bf16[1536,2,256]{2,1,0:T(2,128)(2,1)S(1)}, bf16[1536,2,256]{2,1,0:T(2,128)(2,1)}, u32[]{:S(2)}) copy-start(bf16[1536,2,256]{2,1,0:T(2,128)(2,1)} %param.18) | copy-start | bytes 4718596
  0.0 8.6 %copy-start.21 = (s32[64]{0:T(128)S(1)}, s32[64]{0:T(128)}, u32[]{:S(2)}) copy-start(s32[64]{0:T(128)} %param.22) | copy-start | bytes 772
  1.2 3.4 %collective-permute-start = (bf16[128,2,128]{2,0,1:T(8,128)(2,1)S(1)}, bf16[128,2,128]{2,0,1:T(8,128)(2,1)S(1)}, u32[]{:S(2)}, u32[]{:S(2)}) collective-permute-start(bf16[128,2,128]{2,0,1:T(8,128)(2,1)S(1)} %bitcast.148), channel_id=1, source_target_pairs={{0,16},{4,20},{8,24},{12,28},{16,0},{20,4},{24,8},{28,12},{32,48},... | collective-permute-start | bytes 196616 | tf_op jit(solution)/shard_map/ppermute | solution.py:77
  4.5 20.9 %copy-start.22 = (s32[64]{0:T(128)S(1)}, s32[64]{0:T(128)}, u32[]{:S(2)}) copy-start(s32[64]{0:T(128)} %param.21) | copy-start | bytes 772
  4.6 4.1 %collective-permute-start.1 = (bf16[2,128,2,128]{3,1,2,0:T(8,128)(2,1)S(1)}, bf16[2,128,2,128]{3,1,2,0:T(8,128)(2,1)}, u32[]{:S(2)}, u32[]{:S(2)}) collective-permute-start(bf16[2,128,2,128]{3,1,2,0:T(8,128)(2,1)S(1)} %pad_maximum_fusion.9), channel_id=1, source_target_pairs={{0,4},{4,8},{8,12},{12,0},{16,20},{20,24},{24,28},{28,16},{32,36},... | collective-permute-start | bytes 393224 | tf_op jit(solution)/shard_map/ppermute | solution.py:82
  5.9 5.5 %collective-permute-start.2 = (bf16[2,128,2,128]{3,1,2,0:T(8,128)(2,1)S(1)}, bf16[2,128,2,128]{3,1,2,0:T(8,128)(2,1)}, u32[]{:S(2)}, u32[]{:S(2)}) collective-permute-start(bf16[2,128,2,128]{3,1,2,0:T(8,128)(2,1)S(1)} %pad_maximum_fusion.9), channel_id=1, source_target_pairs={{0,8},{4,12},{8,0},{12,4},{16,24},{20,28},{24,16},{28,20},{32,40},... | collective-permute-start | bytes 393224 | tf_op jit(solution)/shard_map/ppermute | solution.py:82
  6.7 5.9 %collective-permute-start.3 = (bf16[2,128,2,128]{3,1,2,0:T(8,128)(2,1)S(1)}, bf16[2,128,2,128]{3,1,2,0:T(8,128)(2,1)}, u32[]{:S(2)}, u32[]{:S(2)}) collective-permute-start(bf16[2,128,2,128]{3,1,2,0:T(8,128)(2,1)S(1)} %pad_maximum_fusion.9), channel_id=1, source_target_pairs={{0,12},{4,0},{8,4},{12,8},{16,28},{20,16},{24,20},{28,24},{32,44},... | collective-permute-start | bytes 393224 | tf_op jit(solution)/shard_map/ppermute | solution.py:82
  8.6 11.0 %copy-start.4 = (bf16[512,1536]{1,0:T(8,128)(2,1)S(1)}, bf16[512,1536]{1,0:T(8,128)(2,1)}, u32[]{:S(2)}) copy-start(bf16[512,1536]{1,0:T(8,128)(2,1)} %param.15) | copy-start | bytes 4718596
  14.7 12.0 %collective-permute-start.4 = (bf16[4,2,128,2,128]{4,2,3,1,0:T(8,128)(2,1)}, bf16[4,2,128,2,128]{4,2,3,1,0:T(8,128)(2,1)}, u32[]{:S(2)}, u32[]{:S(2)}) collective-permute-start(bf16[4,2,128,2,128]{4,2,3,1,0:T(8,128)(2,1)} %get-tuple-element.21), channel_id=1, source_target_pairs={{0,32},{4,36},{8,40},{12,44},{16,48},{20,52},{24,56},{28,60},{32,6... | collective-permute-start | bytes 1572872 | tf_op jit(solution)/shard_map/ppermute | solution.py:85
  15.8 23.1 %collective-permute-start.5 = (bf16[4,2,128,2,128]{4,2,3,1,0:T(8,128)(2,1)}, bf16[4,2,128,2,128]{4,2,3,1,0:T(8,128)(2,1)}, u32[]{:S(2)}, u32[]{:S(2)}) collective-permute-start(bf16[4,2,128,2,128]{4,2,3,1,0:T(8,128)(2,1)} %get-tuple-element.21), channel_id=1, source_target_pairs={{0,64},{4,68},{8,72},{12,76},{16,80},{20,84},{24,88},{28,92},{32,9... | collective-permute-start | bytes 1572872 | tf_op jit(solution)/shard_map/ppermute | solution.py:85
  18.5 22.4 %collective-permute-start.6 = (bf16[4,2,128,2,128]{4,2,3,1,0:T(8,128)(2,1)}, bf16[4,2,128,2,128]{4,2,3,1,0:T(8,128)(2,1)}, u32[]{:S(2)}, u32[]{:S(2)}) collective-permute-start(bf16[4,2,128,2,128]{4,2,3,1,0:T(8,128)(2,1)} %get-tuple-element.21), channel_id=1, source_target_pairs={{0,96},{4,100},{8,104},{12,108},{16,112},{20,116},{24,120},{28,124... | collective-permute-start | bytes 1572872 | tf_op jit(solution)/shard_map/ppermute | solution.py:85
  19.9 26.1 %copy-start.19 = (f32[1536]{0:T(1024)S(1)}, f32[1536]{0:T(1024)}, u32[]{:S(2)}) copy-start(f32[1536]{0:T(1024)} %param.16) | copy-start | bytes 18436
  19.9 30.5 %collective-permute-start.10 = (bf16[384,1536]{1,0:T(8,128)(2,1)}, bf16[384,1536]{1,0:T(8,128)(2,1)}, u32[]{:S(2)}, u32[]{:S(2)}) collective-permute-start(bf16[384,1536]{1,0:T(8,128)(2,1)} %param.19), channel_id=1, source_target_pairs={{0,16},{1,19},{2,18},{3,17},{4,20},{5,23},{6,22},{7,21},{8,24},{9,... | collective-permute-start | bytes 3538952 | tf_op jit(solution)/shard_map/ppermute | solution.py:66
  25.4 20.6 %copy-start.5 = (bf16[512,1536]{1,0:T(8,128)(2,1)S(1)}, bf16[512,1536]{1,0:T(8,128)(2,1)}, u32[]{:S(2)}) copy-start(bf16[512,1536]{1,0:T(8,128)(2,1)} %param.15) | copy-start | bytes 4718596
  25.4 20.6 %copy-start.18 = (bf16[1536,384]{1,0:T(8,128)(2,1)S(1)}, bf16[1536,384]{1,0:T(8,128)(2,1)}, u32[]{:S(2)}) copy-start(bf16[1536,384]{1,0:T(8,128)(2,1)} %param.17) | copy-start | bytes 3538948
  25.5 36.4 %collective-permute-start.13 = (bf16[1,576,1536]{2,1,0:T(8,128)(2,1)S(1)}, bf16[1,576,1536]{2,1,0:T(8,128)(2,1)}, u32[]{:S(2)}, u32[]{:S(2)}) collective-permute-start(bf16[1,576,1536]{2,1,0:T(8,128)(2,1)S(1)} %bitcast.129), channel_id=1, source_target_pairs={{0,16},{1,19},{2,18},{3,17},{4,20},{5,23},{6,22},{7,21},{8,24},{9,... | collective-permute-start | bytes 5308424 | tf_op jit(solution)/shard_map/ppermute | solution.py:66
  44.0 5.7 %copy-start.17 = (s32[32]{0:T(128)S(1)}, s32[32]{0:T(128)}, u32[]{:S(2)}) copy-start(s32[32]{0:T(128)} %param.23) | copy-start | bytes 388
  44.0 30.9 %collective-permute-start.7 = (bf16[32,128,2,128]{3,1,2,0:T(8,128)(2,1)}, bf16[32,128,2,128]{3,1,2,0:T(8,128)(2,1)}, u32[]{:S(2)}, u32[]{:S(2)}) collective-permute-start(bf16[32,128,2,128]{3,1,2,0:T(8,128)(2,1)} %bitcast.17), channel_id=1, source_target_pairs={{0,1},{1,0},{2,3},{3,2},{4,5},{5,4},{6,7},{7,6},{8,9},{9,8},{10,11... | collective-permute-start | bytes 6291464 | tf_op jit(solution)/shard_map/ppermute | solution.py:43
  50.4 21.2 %collective-permute-start.11 = (bf16[384,1536]{1,0:T(8,128)(2,1)}, bf16[384,1536]{1,0:T(8,128)(2,1)}, u32[]{:S(2)}, u32[]{:S(2)}) collective-permute-start(bf16[384,1536]{1,0:T(8,128)(2,1)} %collective-permute-done.10), channel_id=1, source_target_pairs={{0,18},{1,17},{2,16},{3,19},{4,22},{5,21},{6,20},{7,23},{8,26},{9,... | collective-permute-start | bytes 3538952 | tf_op jit(solution)/shard_map/ppermute | solution.py:67
  61.9 46.2 %collective-permute-start.14 = (bf16[1,576,1536]{2,1,0:T(8,128)(2,1)}, bf16[1,576,1536]{2,1,0:T(8,128)(2,1)}, u32[]{:S(2)}, u32[]{:S(2)}) collective-permute-start(bf16[1,576,1536]{2,1,0:T(8,128)(2,1)} %collective-permute-done.13), channel_id=1, source_target_pairs={{0,18},{1,17},{2,16},{3,19},{4,22},{5,21},{6,20},{7,23},{8,26},{9,... | collective-permute-start | bytes 5308424 | tf_op jit(solution)/shard_map/ppermute | solution.py:67
  74.8 38.7 %collective-permute-start.12 = (bf16[768,1536]{1,0:T(8,128)(2,1)}, bf16[768,1536]{1,0:T(8,128)(2,1)}, u32[]{:S(2)}, u32[]{:S(2)}) collective-permute-start(bf16[768,1536]{1,0:T(8,128)(2,1)} %pad_maximum_fusion.2), channel_id=1, source_target_pairs={{0,1},{1,0},{2,3},{3,2},{4,5},{5,4},{6,7},{7,6},{8,9},{9,8},{10,11... | collective-permute-start | bytes 7077896 | tf_op jit(solution)/shard_map/ppermute | solution.py:43
  94.3 12.5 %collective-permute-start.8 = (bf16[512,384]{0,1:T(8,128)(2,1)S(1)}, bf16[512,384]{0,1:T(8,128)(2,1)S(1)}, u32[]{:S(2)}, u32[]{:S(2)}) collective-permute-start(bf16[512,384]{0,1:T(8,128)(2,1)S(1)} %bitcast.139), channel_id=1, source_target_pairs={{0,2},{1,3},{2,0},{3,1},{4,6},{5,7},{6,4},{7,5},{8,10},{9,11},{10,... | collective-permute-start | bytes 1179656 | tf_op jit(solution)/shard_map/ppermute | solution.py:43
  106.9 6.6 %collective-permute-start.9 = (bf16[512,768]{0,1:T(8,128)(2,1)S(1)}, bf16[512,768]{0,1:T(8,128)(2,1)}, u32[]{:S(2)}, u32[]{:S(2)}) collective-permute-start(bf16[512,768]{0,1:T(8,128)(2,1)S(1)} %pad_maximum_fusion.7), channel_id=1, source_target_pairs={{0,1},{1,0},{2,3},{3,2},{4,5},{5,4},{6,7},{7,6},{8,9},{9,8},{10,11... | collective-permute-start | bytes 2359304 | tf_op jit(solution)/shard_map/ppermute | solution.py:43
  108.1 5.4 %copy-start.7 = (bf16[512,1536]{1,0:T(8,128)(2,1)S(1)}, bf16[512,1536]{1,0:T(8,128)(2,1)}, u32[]{:S(2)}) copy-start(bf16[512,1536]{1,0:T(8,128)(2,1)} %param.15) | copy-start | bytes 4718596
  111.8 16.2 %collective-permute-start.15 = (bf16[2,576,1536]{2,1,0:T(8,128)(2,1)}, bf16[2,576,1536]{2,1,0:T(8,128)(2,1)}, u32[]{:S(2)}, u32[]{:S(2)}) collective-permute-start(bf16[2,576,1536]{2,1,0:T(8,128)(2,1)} %pad_maximum_fusion.1), channel_id=1, source_target_pairs={{0,1},{1,0},{2,3},{3,2},{4,5},{5,4},{6,7},{7,6},{8,9},{9,8},{10,11... | collective-permute-start | bytes 10616840 | tf_op jit(solution)/shard_map/ppermute | solution.py:43
  113.4 5.6 %copy-start.20 = (f32[1536]{0:T(1024)S(1)}, f32[1536]{0:T(1024)}, u32[]{:S(2)}) copy-start(f32[1536]{0:T(1024)} %param.24) | copy-start | bytes 18436
  122.8 47.4 %all-to-all-start = ((bf16[32,32,1536]{2,1,0:T(8,128)(2,1)}), bf16[32,32,1536]{2,1,0:T(8,128)(2,1)}, u32[]{:S(2)}, u32[]{:S(2)}) async-start(bf16[32,32,1536]{2,1,0:T(8,128)(2,1)} %bitcast.134), calls=%async_computation | async-start | bytes 6291456 | tf_op jit(solution)/shard_map/all_to_all | solution.py:210
  187.3 47.3 %all-to-all-start.1 = ((bf16[32,32,1536]{2,1,0:T(8,128)(2,1)}), bf16[32,32,1536]{2,1,0:T(8,128)(2,1)S(1)}, u32[]{:S(2)}, u32[]{:S(2)}) async-start(bf16[32,32,1536]{2,1,0:T(8,128)(2,1)} %bitcast.135), calls=%async_computation.1 | async-start | bytes 6291456 | tf_op jit(solution)/shard_map/all_to_all | solution.py:217
  239.2 5.7 %collective-permute-start.16 = (f32[256,1536]{1,0:T(8,128)}, f32[256,1536]{1,0:T(8,128)}, u32[]{:S(2)}, u32[]{:S(2)}) collective-permute-start(f32[256,1536]{1,0:T(8,128)} %convolution_add_fusion), channel_id=1, source_target_pairs={{0,1},{1,0},{2,3},{3,2},{4,5},{5,4},{6,7},{7,6},{8,9},{9,8},{10,11... | collective-permute-start | bytes 4718600 | tf_op jit(solution)/shard_map/ppermute | solution.py:43
  247.7 21.2 %collective-permute-start.17 = (f32[128,1536]{1,0:T(8,128)}, f32[128,1536]{1,0:T(8,128)}, u32[]{:S(2)}, u32[]{:S(2)}) collective-permute-start(f32[128,1536]{1,0:T(8,128)} %dynamic-slice_add_fusion), channel_id=1, source_target_pairs={{0,2},{1,3},{2,0},{3,1},{4,6},{5,7},{6,4},{7,5},{8,10},{9,11},{10,... | collective-permute-start | bytes 2359304 | tf_op jit(solution)/shard_map/ppermute | solution.py:43
  270.7 11.3 %collective-permute-start.18 = (bf16[128,1536]{1,0:T(8,128)(2,1)S(1)}, bf16[128,1536]{1,0:T(8,128)(2,1)S(1)}, u32[]{:S(2)}, u32[]{:S(2)}) collective-permute-start(bf16[128,1536]{1,0:T(8,128)(2,1)S(1)} %get-tuple-element.12), channel_id=1, source_target_pairs={{0,2},{1,3},{2,0},{3,1},{4,6},{5,7},{6,4},{7,5},{8,10},{9,11},{10,... | collective-permute-start | bytes 1179656 | tf_op jit(solution)/shard_map/ppermute | solution.py:43
  282.0 3.8 %collective-permute-start.19 = (bf16[256,1536]{1,0:T(8,128)(2,1)S(1)}, bf16[256,1536]{1,0:T(8,128)(2,1)S(1)}, u32[]{:S(2)}, u32[]{:S(2)}) collective-permute-start(bf16[256,1536]{1,0:T(8,128)(2,1)S(1)} %constant_dynamic-update-slice_fusion.2), channel_id=1, source_target_pairs={{0,1},{1,0},{2,3},{3,2},{4,5},{5,4},{6,7},{7,6},{8,9},{9,8},{10,11... | collective-permute-start | bytes 2359304 | tf_op jit(solution)/shard_map/ppermute | solution.py:43
  (13 other events, 33.7 us)
where the time goes:
time: 288 us; the launch traced here: 287 us
  waiting for transfers between devices  140 us (49%)
  matrix products  49.8 us (17%)
  starting transfers between devices  43 us (15%)
  other arithmetic  30.5 us (11%)
  local copies, waits for them, and re-layouts  21.6 us (8%)
    all_to_all x1, waiting for transfers between devices, body(): back = lax.all_to_all(part, 'req', split_axis=0, concat_axis=0, tiled=True)  39.6 us
    all_to_all x1, waiting for transfers between devices, body(): lax.all_to_all(send, 'req', split_axis=0, concat_axis=0, tiled=True)  36.2 us
    ppermute x9, waiting for transfers between devices, exp_flip(): return lax.ppermute(x, 'exp', [(e, e ^ bit) for e in range(n_exp)])  35.3 us
    ppermute x9, starting transfers between devices, exp_flip(): return lax.ppermute(x, 'exp', [(e, e ^ bit) for e in range(n_exp)])  17.1 us
    ppermute x3, waiting for transfers between devices, gather_prefix_halves(): lax.ppermute(along_x, 'req', req_shift_pairs(n_req, 'y', d))  15.3 us
    dot_general x1, matrix products, body(): jnp.dot(hidden, down_full, preferred_element_type=jnp.float32)  10.2 us
    ppermute x2, waiting for transfers between devices, far_relay(): return lax.ppermute(hop, ('req', 'exp'), second)  9.51 us
    concatenate x2, other arithmetic, gather_exp_relay(): near = exp_flip(jnp.concatenate([x, far], axis=axis), n_exp, 1)  6.88 us
  transfers between devices with their start and end apart: 22, of which 14 were waited for; matrix products, arithmetic and copies ran while one was open for 25% of the time, Pallas kernels for 0%

commit v1 on v0

--- a/solution.py
+++ b/solution.py
@@ -147,16 +147,14 @@
     in_first = positions < pair[0]
     my_y, my_z, my_x = req_index // 8, (req_index // 4) % 2, req_index % 4
 
-    def prefix_of(group):
-        owner = lax.dynamic_slice_in_dim(owners, group * per_group, per_group, 0)
-        where = ((my_y - owner // 8) % 4) * 8 + ((my_x - owner % 4) % 4) * 2 + (my_z - (owner // 4) % 2) % 2
-        part_mine = halves_mine[where]
-        part_other = halves_other[where]
-        rows = jnp.concatenate([part_mine, part_other], axis=1)
-        return rows.reshape(per_group * 2 * half_rows, 2, HEAD_SIZE)
-
-    prefix_a = prefix_of(pair_groups[0])
-    prefix_b = prefix_of(pair_groups[1])
+    owner = jnp.stack(
+        [lax.dynamic_slice_in_dim(owners, pair_groups[i] * per_group, per_group, 0) for i in range(2)]
+    )
+    where = ((my_y - owner // 8) % 4) * 8 + ((my_x - owner % 4) % 4) * 2 + (my_z - (owner // 4) % 2) % 2
+    rows = jnp.concatenate([halves_mine[where], halves_other[where]], axis=2)
+    rows = rows.reshape(2, per_group * 2 * half_rows, 2, HEAD_SIZE)
+    prefix_a = rows[0]
+    prefix_b = rows[1]
     zero_q = jnp.zeros_like(query_rows)
     first3 = in_first[:, None, None]
     query_ab = jnp.concatenate(

time: 288 us -> 299 us (1.038)
  waiting for transfers between devices: 140 us -> 153 us
  local copies, waits for them, and re-layouts: 21.6 us -> 16 us
    ppermute x2, waiting for transfers between devices: 0.01 us -> 17.7 us  [far_relay(): hop = lax.ppermute(x, ('req', 'exp'), first)]
    ppermute x2, waiting for transfers between devices: 9.51 us -> 0.01 us  [far_relay(): return lax.ppermute(hop, ('req', 'exp'), second)]
    ppermute x9, waiting for transfers between devices: 35.3 us -> 40.3 us  [exp_flip(): return lax.ppermute(x, 'exp', [(e, e ^ bit) for e in range(n_exp)])]
    gather x4 -> x2, local copies, waits for them, and re-layouts: 10.5 us -> 5.58 us  [body(): rows = jnp.concatenate([halves_mine[where], halves_other[where]], axis=2)]
    ppermute x2, starting transfers between devices: 3.57 us -> 6.98 us  [far_relay(): hop = lax.ppermute(x, ('req', 'exp'), first)]
  transfers between devices with their start and end apart: 22 -> 22, of which waited for: 14 -> 14; matrix products, arithmetic and copies ran while one was open for 25% -> 23% of each run, Pallas kernels for 0% -> 0%
where the time goes in v1:
time: 299 us; the launch traced here: 298 us
  waiting for transfers between devices  153 us (51%)
  matrix products  51.5 us (17%)
  starting transfers between devices  44.3 us (15%)
  other arithmetic  30.6 us (10%)
  local copies, waits for them, and re-layouts  16 us (5%)
    ppermute x9, waiting for transfers between devices, exp_flip(): return lax.ppermute(x, 'exp', [(e, e ^ bit) for e in range(n_exp)])  40.3 us
    all_to_all x1, waiting for transfers between devices, body(): back = lax.all_to_all(part, 'req', split_axis=0, concat_axis=0, tiled=True)  39.8 us
    all_to_all x1, waiting for transfers between devices, body(): lax.all_to_all(send, 'req', split_axis=0, concat_axis=0, tiled=True)  36.2 us
    ppermute x2, waiting for transfers between devices, far_relay(): hop = lax.ppermute(x, ('req', 'exp'), first)  17.7 us
    ppermute x3, waiting for transfers between devices, gather_prefix_halves(): lax.ppermute(along_x, 'req', req_shift_pairs(n_req, 'y', d))  15.4 us
    ppermute x9, starting transfers between devices, exp_flip(): return lax.ppermute(x, 'exp', [(e, e ^ bit) for e in range(n_exp)])  14.7 us
    dot_general x1, matrix products, body(): jnp.dot(hidden, down_full, preferred_element_type=jnp.float32)  10.2 us
    all_to_all x1, starting transfers between devices, body(): lax.all_to_all(send, 'req', split_axis=0, concat_axis=0, tiled=True)  7 us
  transfers between devices with their start and end apart: 22, of which 14 were waited for; matrix products, arithmetic and copies ran while one was open for 23% of the time, Pallas kernels for 0%

profile of v1, /device:TPU:3, one launch (start us, length us, event | category | flops | bytes accessed | tf_op | source)
XLA Modules:
  0.0 297.7 jit_solution(16418418909280189741)
XLA Ops:
  8.7 2.7 collective-permute-done.2
  15.8 2.6 collective-permute-start.5
  20.0 3.5 %collective-permute-start.10 = (bf16[384,1536]{1,0:T(8,128)(2,1)}, bf16[384,1536]{1,0:T(8,128)(2,1)}, u32[]{:S(2)}, u32[]{:S(2)}) collective-permute-start(bf16[384,1536]{1,0:T(8,128)(2,1)} %param.19), channel_id=1, source_target_pairs={{0,16},{1,19},{2,18},{3,17},{4,20},{5,23},{6,22},{7,21},{8,24},{9,... | collective-permute-start | bytes 3538952 | tf_op jit(solution)/shard_map/ppermute | solution.py:66
  26.7 12.3 %collective-permute-done.5 = bf16[4,2,128,2,128]{4,2,3,1,0:T(8,128)(2,1)} collective-permute-done((bf16[4,2,128,2,128]{4,2,3,1,0:T(8,128)(2,1)}, bf16[4,2,128,2,128]{4,2,3,1,0:T(8,128)(2,1)}, u32[]{:S(2)}, u32[]{:S(2)}) %collective-permute-start.5) | collective-permute-done | bytes 524320 | tf_op jit(solution)/shard_map/ppermute | solution.py:85
  40.8 3.1 %pad_maximum_fusion.3 = bf16[4,4,2,128,2,128]{5,3,4,2,1,0:T(8,128)(2,1)} fusion(bf16[1,4,2,128,2,128]{5,3,4,2,1,0:T(8,128)(2,1)} %bitcast.16, bf16[1,4,2,128,2,128]{5,3,4,2,1,0:T(8,128)(2,1)} %bitcast.15, bf16[1,4,2,128,2,128]{5,3,4,2,1,0:T(8,128)(2,1)} %bitcast.14, bf16[1,4,2,128,2,128]{5,3,4,2,1,0:T(8,128)(2,1)} %get-tuple-element.22), kind=kLoop, calls=%fused_computation.43 | loop fusion | flops 3145728 | bytes 4194304 | tf_op jit(solution)/shard_map/stack | solution.py:84
  46.3 3.5 %collective-permute-start.13 = (bf16[1,576,1536]{2,1,0:T(8,128)(2,1)S(1)}, bf16[1,576,1536]{2,1,0:T(8,128)(2,1)}, u32[]{:S(2)}, u32[]{:S(2)}) collective-permute-start(bf16[1,576,1536]{2,1,0:T(8,128)(2,1)S(1)} %bitcast.135), channel_id=1, source_target_pairs={{0,16},{1,19},{2,18},{3,17},{4,20},{5,23},{6,22},{7,21},{8,24},{9,... | collective-permute-start | bytes 5308424 | tf_op jit(solution)/shard_map/ppermute | solution.py:66
  49.8 3.4 %fusion.35 = bf16[512,384]{0,1:T(8,128)(2,1)} fusion(bf16[1536,384]{1,0:T(8,128)(2,1)} %param.17, bf16[512,1536]{1,0:T(8,128)(2,1)} %param.15, f32[1536]{0:T(1024)S(1)} %copy-done.23, f32[512]{0:T(512)S(1)} %add_rsqrt_fusion.1), kind=kOutput, calls=%fused_computation.61 | convolution fusion | flops 607518720 | bytes 3153920 | tf_op jit(solution)/shard_map/dot_general | solution.py:135
  59.2 2.2 fusion.19
  61.5 2.3 gather_fusion
  63.8 17.7 %collective-permute-done.13 = bf16[1,576,1536]{2,1,0:T(8,128)(2,1)} collective-permute-done((bf16[1,576,1536]{2,1,0:T(8,128)(2,1)S(1)}, bf16[1,576,1536]{2,1,0:T(8,128)(2,1)}, u32[]{:S(2)}, u32[]{:S(2)}) %collective-permute-start.13) | collective-permute-done | bytes 1769504 | tf_op jit(solution)/shard_map/ppermute | solution.py:66
  81.5 3.2 %pad_maximum_fusion.2 = bf16[768,1536]{1,0:T(8,128)(2,1)} fusion(bf16[384,1536]{1,0:T(8,128)(2,1)} %collective-permute-done.11, bf16[384,1536]{1,0:T(8,128)(2,1)} %param.19), kind=kLoop, calls=%fused_computation.42 | loop fusion | flops 4718592 | bytes 4718592 | tf_op jit(solution)/shard_map/concatenate | solution.py:72
  84.7 3.9 %collective-permute-start.12 = (bf16[768,1536]{1,0:T(8,128)(2,1)}, bf16[768,1536]{1,0:T(8,128)(2,1)}, u32[]{:S(2)}, u32[]{:S(2)}) collective-permute-start(bf16[768,1536]{1,0:T(8,128)(2,1)} %pad_maximum_fusion.2), channel_id=1, source_target_pairs={{0,1},{1,0},{2,3},{3,2},{4,5},{5,4},{6,7},{7,6},{8,9},{9,8},{10,11... | collective-permute-start | bytes 7077896 | tf_op jit(solution)/shard_map/ppermute | solution.py:43
  88.5 3.2 %gather_fusion.1 = bf16[16,128,2,128]{3,1,2,0:T(8,128)(2,1)} fusion(bf16[32,128,2,128]{3,1,2,0:T(8,128)(2,1)} %collective-permute-done.7, s32[1024]{0:T(1024)S(1)} %pad_clamp_fusion), kind=kCustom, calls=%fused_computation.1 | custom fusion | bytes 2097216 | tf_op jit(solution)/shard_map/gather | solution.py:154
  98.8 3.5 %fusion.32 = f32[512,3,256]{2,0,1:T(8,128)S(1)} fusion(f32[2048,512,3]{1,0,2:T(8,128)S(1)} %get-tuple-element.33, f32[3,512]{1,0:T(4,128)S(1)} %add.242, f32[3,512]{1,0:T(4,128)S(1)} %max.14, bf16[2048,128]{1,0:T(8,128)(2,1)S(1)} %copy-done.13, bf16[2048,128]{1,0:T(8,128)(2,1)S(1)} %copy-done.14), kind=kOutput, calls=%fused_computation.57 | convolution fusion | flops 1622147072 | bytes 15216640 | tf_op jit(solution)/shard_map/htp,pd->thd/dot_general | solution.py:179
  104.4 11.4 %collective-permute-done.8 = bf16[512,384]{0,1:T(8,128)(2,1)S(1)} collective-permute-done((bf16[512,384]{0,1:T(8,128)(2,1)S(1)}, bf16[512,384]{0,1:T(8,128)(2,1)S(1)}, u32[]{:S(2)}, u32[]{:S(2)}) %collective-permute-start.8) | collective-permute-done | bytes 393248 | tf_op jit(solution)/shard_map/ppermute | solution.py:43
  117.8 3.7 %pad_maximum_fusion.1 = bf16[2,576,1536]{2,1,0:T(8,128)(2,1)} fusion(bf16[1,576,1536]{2,1,0:T(8,128)(2,1)} %collective-permute-done.14, bf16[1,576,1536]{2,1,0:T(8,128)(2,1)S(1)} %bitcast.136), kind=kLoop, calls=%fused_computation.25 | loop fusion | flops 1769472 | bytes 7077888 | tf_op jit(solution)/shard_map/concatenate | solution.py:72
  123.2 5.5 %fusion.10 = (f32[512]{0:T(512)S(1)}, bf16[512,1536]{1,0:T(8,128)(2,1)S(1)}) fusion(bf16[768,1536]{1,0:T(8,128)(2,1)} %collective-permute-done.12, bf16[384,1536]{1,0:T(8,128)(2,1)} %collective-permute-done.11, bf16[384,1536]{1,0:T(8,128)(2,1)} %param.19, bf16[512,768]{0,1:T(8,128)(2,1)} %collective-permute-done.9, bf16[512,384]{0,1:T(8,128)(2,1)S(1)} %copy-done.16, ...), kind=kOutput, calls=%fused_computation.26 | convolution fusion | flops 2439511552 | bytes 9439232 | tf_op jit(solution)/shard_map/dot_general | solution.py:187
  128.8 3.8 %convolution_convert_fusion.1 = bf16[1024,1536]{1,0:T(8,128)(2,1)} fusion(pred[512,1024]{1,0:T(8,128)(4,1)S(1)} %fusion.2, bf16[512,1536]{1,0:T(8,128)(2,1)S(1)} %get-tuple-element.37, f32[1536]{0:T(1024)S(1)} %copy-done.24, f32[512]{0:T(512)S(1)} %add_rsqrt_fusion), kind=kOutput, calls=%fused_computation.24 | convolution fusion | flops 1615331328 | bytes 5251072 | tf_op jit(solution)/shard_map/tq,td->qd/dot_general | solution.py:206
  132.5 7.0 %all-to-all-start = ((bf16[32,32,1536]{2,1,0:T(8,128)(2,1)}), bf16[32,32,1536]{2,1,0:T(8,128)(2,1)}, u32[]{:S(2)}, u32[]{:S(2)}) async-start(bf16[32,32,1536]{2,1,0:T(8,128)(2,1)} %bitcast.142), calls=%async_computation | async-start | bytes 6291456 | tf_op jit(solution)/shard_map/all_to_all | solution.py:208
  139.5 3.4 %pad_maximum_fusion = bf16[4,576,1536]{2,1,0:T(8,128)(2,1)S(1)} fusion(bf16[2,576,1536]{2,1,0:T(8,128)(2,1)} %collective-permute-done.15, bf16[1,576,1536]{2,1,0:T(8,128)(2,1)} %collective-permute-done.14, bf16[1,576,1536]{2,1,0:T(8,128)(2,1)S(1)} %bitcast.137), kind=kLoop, calls=%fused_computation.10 | loop fusion | flops 7077888 | bytes 14155776 | tf_op jit(solution)/shard_map/concatenate | solution.py:73
  143.0 2.6 fusion.81
  145.6 36.2 %all-to-all-done = bf16[32,32,1536]{2,1,0:T(8,128)(2,1)} async-done(((bf16[32,32,1536]{2,1,0:T(8,128)(2,1)}), bf16[32,32,1536]{2,1,0:T(8,128)(2,1)}, u32[]{:S(2)}, u32[]{:S(2)}) %all-to-all-start) | async-done | bytes 3145760 | tf_op jit(solution)/shard_map/all_to_all | solution.py:208
  181.8 6.9 %fusion.83 = f32[1024,768]{1,0:T(8,128)} fusion(bf16[1024,1536]{1,0:T(8,128)(2,1)} %bitcast.44, bf16[768,1536]{1,0:T(8,128)(2,1)} %bitcast.146), kind=kOutput, calls=%fused_computation.170 | convolution fusion | flops 2415919104 | bytes 8650752 | tf_op jit(solution)/shard_map/dot_general | solution.py:210
  188.7 10.2 %convolution_convert_fusion = bf16[1024,1536]{1,0:T(8,128)(2,1)} fusion(bf16[768,1536]{1,0:T(8,128)(2,1)} %bitcast.145, f32[1024,768]{1,0:T(8,128)} %fusion.83, bf16[1024,1536]{1,0:T(8,128)(2,1)} %bitcast.44, bf16[768,1536]{1,0:T(8,128)(2,1)S(1)} %bitcast.144), kind=kOutput, calls=%fused_computation.23 | convolution fusion | flops 4835770368 | bytes 14155776 | tf_op jit(solution)/shard_map/dot_general | solution.py:213
  198.9 5.0 %all-to-all-start.1 = ((bf16[32,32,1536]{2,1,0:T(8,128)(2,1)}), bf16[32,32,1536]{2,1,0:T(8,128)(2,1)S(1)}, u32[]{:S(2)}, u32[]{:S(2)}) async-start(bf16[32,32,1536]{2,1,0:T(8,128)(2,1)} %bitcast.143), calls=%async_computation.1 | async-start | bytes 6291456 | tf_op jit(solution)/shard_map/all_to_all | solution.py:215
  203.9 2.7 select_reduce_fusion
  206.5 39.8 %all-to-all-done.1 = bf16[32,32,1536]{2,1,0:T(8,128)(2,1)S(1)} async-done(((bf16[32,32,1536]{2,1,0:T(8,128)(2,1)}), bf16[32,32,1536]{2,1,0:T(8,128)(2,1)S(1)}, u32[]{:S(2)}, u32[]{:S(2)}) %all-to-all-start.1) | async-done | bytes 3145760 | tf_op jit(solution)/shard_map/all_to_all | solution.py:215
  246.3 2.3 fusion.54
  250.8 2.2 collective-permute-start.16
  256.4 2.8 dynamic-slice_add_fusion
  264.0 15.8 %collective-permute-done.17 = f32[128,1536]{1,0:T(8,128)} collective-permute-done((f32[128,1536]{1,0:T(8,128)}, f32[128,1536]{1,0:T(8,128)}, u32[]{:S(2)}, u32[]{:S(2)}) %collective-permute-start.17) | collective-permute-done | bytes 786464 | tf_op jit(solution)/shard_map/ppermute | solution.py:43
  283.1 9.5 %collective-permute-done.18 = bf16[128,1536]{1,0:T(8,128)(2,1)S(1)} collective-permute-done((bf16[128,1536]{1,0:T(8,128)(2,1)S(1)}, bf16[128,1536]{1,0:T(8,128)(2,1)S(1)}, u32[]{:S(2)}, u32[]{:S(2)}) %collective-permute-start.18) | collective-permute-done | bytes 393248 | tf_op jit(solution)/shard_map/ppermute | solution.py:43
  (131 shorter events, 57.7 us)
Async XLA Ops:
  0.0 55.2 %copy-start = (bf16[1536,2,256]{2,1,0:T(2,128)(2,1)S(1)}, bf16[1536,2,256]{2,1,0:T(2,128)(2,1)}, u32[]{:S(2)}) copy-start(bf16[1536,2,256]{2,1,0:T(2,128)(2,1)} %param.18) | copy-start | bytes 4718596
  0.0 8.6 %copy-start.25 = (s32[64]{0:T(128)S(1)}, s32[64]{0:T(128)}, u32[]{:S(2)}) copy-start(s32[64]{0:T(128)} %param.22) | copy-start | bytes 772
  1.2 3.4 %collective-permute-start = (bf16[128,2,128]{2,0,1:T(8,128)(2,1)S(1)}, bf16[128,2,128]{2,0,1:T(8,128)(2,1)S(1)}, u32[]{:S(2)}, u32[]{:S(2)}) collective-permute-start(bf16[128,2,128]{2,0,1:T(8,128)(2,1)S(1)} %bitcast.156), channel_id=1, source_target_pairs={{0,16},{4,20},{8,24},{12,28},{16,0},{20,4},{24,8},{28,12},{32,48},... | collective-permute-start | bytes 196616 | tf_op jit(solution)/shard_map/ppermute | solution.py:77
  4.6 4.1 %collective-permute-start.1 = (bf16[2,128,2,128]{3,1,2,0:T(8,128)(2,1)S(1)}, bf16[2,128,2,128]{3,1,2,0:T(8,128)(2,1)}, u32[]{:S(2)}, u32[]{:S(2)}) collective-permute-start(bf16[2,128,2,128]{3,1,2,0:T(8,128)(2,1)S(1)} %pad_maximum_fusion.8), channel_id=1, source_target_pairs={{0,4},{4,8},{8,12},{12,0},{16,20},{20,24},{24,28},{28,16},{32,36},... | collective-permute-start | bytes 393224 | tf_op jit(solution)/shard_map/ppermute | solution.py:82
  5.9 5.5 %collective-permute-start.2 = (bf16[2,128,2,128]{3,1,2,0:T(8,128)(2,1)S(1)}, bf16[2,128,2,128]{3,1,2,0:T(8,128)(2,1)}, u32[]{:S(2)}, u32[]{:S(2)}) collective-permute-start(bf16[2,128,2,128]{3,1,2,0:T(8,128)(2,1)S(1)} %pad_maximum_fusion.8), channel_id=1, source_target_pairs={{0,8},{4,12},{8,0},{12,4},{16,24},{20,28},{24,16},{28,20},{32,40},... | collective-permute-start | bytes 393224 | tf_op jit(solution)/shard_map/ppermute | solution.py:82
  6.7 5.9 %collective-permute-start.3 = (bf16[2,128,2,128]{3,1,2,0:T(8,128)(2,1)S(1)}, bf16[2,128,2,128]{3,1,2,0:T(8,128)(2,1)}, u32[]{:S(2)}, u32[]{:S(2)}) collective-permute-start(bf16[2,128,2,128]{3,1,2,0:T(8,128)(2,1)S(1)} %pad_maximum_fusion.8), channel_id=1, source_target_pairs={{0,12},{4,0},{8,4},{12,8},{16,28},{20,16},{24,20},{28,24},{32,44},... | collective-permute-start | bytes 393224 | tf_op jit(solution)/shard_map/ppermute | solution.py:82
  8.6 11.0 %copy-start.4 = (bf16[512,1536]{1,0:T(8,128)(2,1)S(1)}, bf16[512,1536]{1,0:T(8,128)(2,1)}, u32[]{:S(2)}) copy-start(bf16[512,1536]{1,0:T(8,128)(2,1)} %param.15) | copy-start | bytes 4718596
  14.7 12.0 %collective-permute-start.4 = (bf16[4,2,128,2,128]{4,2,3,1,0:T(8,128)(2,1)}, bf16[4,2,128,2,128]{4,2,3,1,0:T(8,128)(2,1)}, u32[]{:S(2)}, u32[]{:S(2)}) collective-permute-start(bf16[4,2,128,2,128]{4,2,3,1,0:T(8,128)(2,1)} %get-tuple-element.23), channel_id=1, source_target_pairs={{0,32},{4,36},{8,40},{12,44},{16,48},{20,52},{24,56},{28,60},{32,6... | collective-permute-start | bytes 1572872 | tf_op jit(solution)/shard_map/ppermute | solution.py:85
  15.8 23.1 %collective-permute-start.5 = (bf16[4,2,128,2,128]{4,2,3,1,0:T(8,128)(2,1)}, bf16[4,2,128,2,128]{4,2,3,1,0:T(8,128)(2,1)}, u32[]{:S(2)}, u32[]{:S(2)}) collective-permute-start(bf16[4,2,128,2,128]{4,2,3,1,0:T(8,128)(2,1)} %get-tuple-element.23), channel_id=1, source_target_pairs={{0,64},{4,68},{8,72},{12,76},{16,80},{20,84},{24,88},{28,92},{32,9... | collective-permute-start | bytes 1572872 | tf_op jit(solution)/shard_map/ppermute | solution.py:85
  18.5 22.4 %collective-permute-start.6 = (bf16[4,2,128,2,128]{4,2,3,1,0:T(8,128)(2,1)}, bf16[4,2,128,2,128]{4,2,3,1,0:T(8,128)(2,1)}, u32[]{:S(2)}, u32[]{:S(2)}) collective-permute-start(bf16[4,2,128,2,128]{4,2,3,1,0:T(8,128)(2,1)} %get-tuple-element.23), channel_id=1, source_target_pairs={{0,96},{4,100},{8,104},{12,108},{16,112},{20,116},{24,120},{28,124... | collective-permute-start | bytes 1572872 | tf_op jit(solution)/shard_map/ppermute | solution.py:85
  19.9 26.1 %copy-start.22 = (s32[32]{0:T(128)S(1)}, s32[32]{0:T(128)}, u32[]{:S(2)}) copy-start(s32[32]{0:T(128)} %param.23) | copy-start | bytes 388
  19.9 26.3 %copy-start.26 = (s32[64]{0:T(128)S(1)}, s32[64]{0:T(128)}, u32[]{:S(2)}) copy-start(s32[64]{0:T(128)} %param.21) | copy-start | bytes 772
  19.9 29.8 %copy-start.23 = (f32[1536]{0:T(1024)S(1)}, f32[1536]{0:T(1024)}, u32[]{:S(2)}) copy-start(f32[1536]{0:T(1024)} %param.16) | copy-start | bytes 18436
  20.0 35.8 %collective-permute-start.10 = (bf16[384,1536]{1,0:T(8,128)(2,1)}, bf16[384,1536]{1,0:T(8,128)(2,1)}, u32[]{:S(2)}, u32[]{:S(2)}) collective-permute-start(bf16[384,1536]{1,0:T(8,128)(2,1)} %param.19), channel_id=1, source_target_pairs={{0,16},{1,19},{2,18},{3,17},{4,20},{5,23},{6,22},{7,21},{8,24},{9,... | collective-permute-start | bytes 3538952 | tf_op jit(solution)/shard_map/ppermute | solution.py:66
  44.0 44.6 %collective-permute-start.7 = (bf16[32,128,2,128]{3,1,2,0:T(8,128)(2,1)}, bf16[32,128,2,128]{3,1,2,0:T(8,128)(2,1)}, u32[]{:S(2)}, u32[]{:S(2)}) collective-permute-start(bf16[32,128,2,128]{3,1,2,0:T(8,128)(2,1)} %bitcast.17), channel_id=1, source_target_pairs={{0,1},{1,0},{2,3},{3,2},{4,5},{5,4},{6,7},{7,6},{8,9},{9,8},{10,11... | collective-permute-start | bytes 6291464 | tf_op jit(solution)/shard_map/ppermute | solution.py:43
  46.3 35.2 %collective-permute-start.13 = (bf16[1,576,1536]{2,1,0:T(8,128)(2,1)S(1)}, bf16[1,576,1536]{2,1,0:T(8,128)(2,1)}, u32[]{:S(2)}, u32[]{:S(2)}) collective-permute-start(bf16[1,576,1536]{2,1,0:T(8,128)(2,1)S(1)} %bitcast.135), channel_id=1, source_target_pairs={{0,16},{1,19},{2,18},{3,17},{4,20},{5,23},{6,22},{7,21},{8,24},{9,... | collective-permute-start | bytes 5308424 | tf_op jit(solution)/shard_map/ppermute | solution.py:66
  55.8 25.7 %collective-permute-start.11 = (bf16[384,1536]{1,0:T(8,128)(2,1)}, bf16[384,1536]{1,0:T(8,128)(2,1)}, u32[]{:S(2)}, u32[]{:S(2)}) collective-permute-start(bf16[384,1536]{1,0:T(8,128)(2,1)} %collective-permute-done.10), channel_id=1, source_target_pairs={{0,18},{1,17},{2,16},{3,19},{4,22},{5,21},{6,20},{7,23},{8,26},{9,... | collective-permute-start | bytes 3538952 | tf_op jit(solution)/shard_map/ppermute | solution.py:67
  81.5 36.3 %collective-permute-start.14 = (bf16[1,576,1536]{2,1,0:T(8,128)(2,1)}, bf16[1,576,1536]{2,1,0:T(8,128)(2,1)}, u32[]{:S(2)}, u32[]{:S(2)}) collective-permute-start(bf16[1,576,1536]{2,1,0:T(8,128)(2,1)} %collective-permute-done.13), channel_id=1, source_target_pairs={{0,18},{1,17},{2,16},{3,19},{4,22},{5,21},{6,20},{7,23},{8,26},{9,... | collective-permute-start | bytes 5308424 | tf_op jit(solution)/shard_map/ppermute | solution.py:67
  84.7 38.5 %collective-permute-start.12 = (bf16[768,1536]{1,0:T(8,128)(2,1)}, bf16[768,1536]{1,0:T(8,128)(2,1)}, u32[]{:S(2)}, u32[]{:S(2)}) collective-permute-start(bf16[768,1536]{1,0:T(8,128)(2,1)} %pad_maximum_fusion.2), channel_id=1, source_target_pairs={{0,1},{1,0},{2,3},{3,2},{4,5},{5,4},{6,7},{7,6},{8,9},{9,8},{10,11... | collective-permute-start | bytes 7077896 | tf_op jit(solution)/shard_map/ppermute | solution.py:43
  103.6 14.2 %copy-start.8 = (bf16[512,3,128]{0,2,1:T(8,128)(2,1)}, bf16[512,3,128]{0,2,1:T(8,128)(2,1)S(1)}, u32[]{:S(2)}) copy-start(bf16[512,3,128]{0,2,1:T(8,128)(2,1)S(1)} %copy.61) | copy-start | bytes 1179652
  103.6 12.3 %collective-permute-start.8 = (bf16[512,384]{0,1:T(8,128)(2,1)S(1)}, bf16[512,384]{0,1:T(8,128)(2,1)S(1)}, u32[]{:S(2)}, u32[]{:S(2)}) collective-permute-start(bf16[512,384]{0,1:T(8,128)(2,1)S(1)} %bitcast.147), channel_id=1, source_target_pairs={{0,2},{1,3},{2,0},{3,1},{4,6},{5,7},{6,4},{7,5},{8,10},{9,11},{10,... | collective-permute-start | bytes 1179656 | tf_op jit(solution)/shard_map/ppermute | solution.py:43
  116.8 6.3 %collective-permute-start.9 = (bf16[512,768]{0,1:T(8,128)(2,1)}, bf16[512,768]{0,1:T(8,128)(2,1)}, u32[]{:S(2)}, u32[]{:S(2)}) collective-permute-start(bf16[512,768]{0,1:T(8,128)(2,1)} %pad_maximum_fusion.6), channel_id=1, source_target_pairs={{0,1},{1,0},{2,3},{3,2},{4,5},{5,4},{6,7},{7,6},{8,9},{9,8},{10,11... | collective-permute-start | bytes 2359304 | tf_op jit(solution)/shard_map/ppermute | solution.py:43
  117.8 5.4 %copy-start.6 = (bf16[512,1536]{1,0:T(8,128)(2,1)S(1)}, bf16[512,1536]{1,0:T(8,128)(2,1)}, u32[]{:S(2)}) copy-start(bf16[512,1536]{1,0:T(8,128)(2,1)} %param.15) | copy-start | bytes 4718596
  117.8 5.4 %copy-start.9 = (bf16[512,3,128]{0,2,1:T(8,128)(2,1)S(1)}, bf16[512,3,128]{0,2,1:T(8,128)(2,1)}, u32[]{:S(2)}) copy-start(bf16[512,3,128]{0,2,1:T(8,128)(2,1)} %copy-done.8) | copy-start | bytes 1179652
  121.6 18.0 %collective-permute-start.15 = (bf16[2,576,1536]{2,1,0:T(8,128)(2,1)}, bf16[2,576,1536]{2,1,0:T(8,128)(2,1)}, u32[]{:S(2)}, u32[]{:S(2)}) collective-permute-start(bf16[2,576,1536]{2,1,0:T(8,128)(2,1)} %pad_maximum_fusion.1), channel_id=1, source_target_pairs={{0,1},{1,0},{2,3},{3,2},{4,5},{5,4},{6,7},{7,6},{8,9},{9,8},{10,11... | collective-permute-start | bytes 10616840 | tf_op jit(solution)/shard_map/ppermute | solution.py:43
  123.2 5.6 %copy-start.24 = (f32[1536]{0:T(1024)S(1)}, f32[1536]{0:T(1024)}, u32[]{:S(2)}) copy-start(f32[1536]{0:T(1024)} %param.24) | copy-start | bytes 18436
  132.5 49.3 %all-to-all-start = ((bf16[32,32,1536]{2,1,0:T(8,128)(2,1)}), bf16[32,32,1536]{2,1,0:T(8,128)(2,1)}, u32[]{:S(2)}, u32[]{:S(2)}) async-start(bf16[32,32,1536]{2,1,0:T(8,128)(2,1)} %bitcast.142), calls=%async_computation | async-start | bytes 6291456 | tf_op jit(solution)/shard_map/all_to_all | solution.py:208
  198.9 47.4 %all-to-all-start.1 = ((bf16[32,32,1536]{2,1,0:T(8,128)(2,1)}), bf16[32,32,1536]{2,1,0:T(8,128)(2,1)S(1)}, u32[]{:S(2)}, u32[]{:S(2)}) async-start(bf16[32,32,1536]{2,1,0:T(8,128)(2,1)} %bitcast.143), calls=%async_computation.1 | async-start | bytes 6291456 | tf_op jit(solution)/shard_map/all_to_all | solution.py:215
  250.8 5.6 %collective-permute-start.16 = (f32[256,1536]{1,0:T(8,128)}, f32[256,1536]{1,0:T(8,128)}, u32[]{:S(2)}, u32[]{:S(2)}) collective-permute-start(f32[256,1536]{1,0:T(8,128)} %convolution_add_fusion), channel_id=1, source_target_pairs={{0,1},{1,0},{2,3},{3,2},{4,5},{5,4},{6,7},{7,6},{8,9},{9,8},{10,11... | collective-permute-start | bytes 4718600 | tf_op jit(solution)/shard_map/ppermute | solution.py:43
  259.3 20.5 %collective-permute-start.17 = (f32[128,1536]{1,0:T(8,128)}, f32[128,1536]{1,0:T(8,128)}, u32[]{:S(2)}, u32[]{:S(2)}) collective-permute-start(f32[128,1536]{1,0:T(8,128)} %dynamic-slice_add_fusion), channel_id=1, source_target_pairs={{0,2},{1,3},{2,0},{3,1},{4,6},{5,7},{6,4},{7,5},{8,10},{9,11},{10,... | collective-permute-start | bytes 2359304 | tf_op jit(solution)/shard_map/ppermute | solution.py:43
  281.6 11.0 %collective-permute-start.18 = (bf16[128,1536]{1,0:T(8,128)(2,1)S(1)}, bf16[128,1536]{1,0:T(8,128)(2,1)S(1)}, u32[]{:S(2)}, u32[]{:S(2)}) collective-permute-start(bf16[128,1536]{1,0:T(8,128)(2,1)S(1)} %get-tuple-element.12), channel_id=1, source_target_pairs={{0,2},{1,3},{2,0},{3,1},{4,6},{5,7},{6,4},{7,5},{8,10},{9,11},{10,... | collective-permute-start | bytes 1179656 | tf_op jit(solution)/shard_map/ppermute | solution.py:43
  292.6 4.1 %collective-permute-start.19 = (bf16[256,1536]{1,0:T(8,128)(2,1)S(1)}, bf16[256,1536]{1,0:T(8,128)(2,1)S(1)}, u32[]{:S(2)}, u32[]{:S(2)}) collective-permute-start(bf16[256,1536]{1,0:T(8,128)(2,1)S(1)} %constant_dynamic-update-slice_fusion.2), channel_id=1, source_target_pairs={{0,1},{1,0},{2,3},{3,2},{4,5},{5,4},{6,7},{7,6},{8,9},{9,8},{10,11... | collective-permute-start | bytes 2359304 | tf_op jit(solution)/shard_map/ppermute | solution.py:43
  (17 other events, 44.8 us)

commit v2 on v0

--- a/solution.py
+++ b/solution.py
@@ -121,7 +121,8 @@
     along_z = gather_prefix_near(mine, n_req)
     ff_shard = w_gate.shape[2]
     packed = jnp.concatenate([w_gate[0].T, w_up[0].T, w_down[0]], axis=0)
-    w_output_late, packed_late, along_z = lax.optimization_barrier((w_output, packed, along_z))
+    packed_late, along_z = lax.optimization_barrier((packed, along_z))
+    w_output_late = w_output
     halves_mine = gather_prefix_halves(along_z, n_req)
     halves_other = exp_flip(halves_mine, n_exp, 1)
     w_output_full = gather_exp_relay(w_output_late, 0, n_req, n_exp)

time: 288 us -> 287 us (level)
  waiting for transfers between devices: 140 us -> 133 us
  starting transfers between devices: 43 us -> 49 us
    ppermute x2, waiting for transfers between devices: 9.51 us -> 4.04 us  [far_relay(): return lax.ppermute(hop, ('req', 'exp'), second)]
    ppermute x3, waiting for transfers between devices: 3.91 us -> 0.33 us  [gather_prefix_halves(): lax.ppermute(along_z, 'req', req_shift_pairs(n_req, 'x', d))]
    ppermute x2, starting transfers between devices: 3.57 us -> 6.9 us  [far_relay(): hop = lax.ppermute(x, ('req', 'exp'), first)]
  transfers between devices with their start and end apart: 22 -> 22, of which waited for: 14 -> 13; matrix products, arithmetic and copies ran while one was open for 25% -> 26% of each run, Pallas kernels for 0% -> 0%
where the time goes in v2:
time: 287 us; the launch traced here: 286 us
  waiting for transfers between devices  133 us (46%)
  matrix products  49.8 us (17%)
  starting transfers between devices  49 us (17%)
  other arithmetic  30.6 us (11%)
  local copies, waits for them, and re-layouts  21.6 us (8%)
    all_to_all x1, waiting for transfers between devices, body(): back = lax.all_to_all(part, 'req', split_axis=0, concat_axis=0, tiled=True)  39.8 us
    ppermute x9, waiting for transfers between devices, exp_flip(): return lax.ppermute(x, 'exp', [(e, e ^ bit) for e in range(n_exp)])  36.9 us
    all_to_all x1, waiting for transfers between devices, body(): lax.all_to_all(send, 'req', split_axis=0, concat_axis=0, tiled=True)  36.2 us
    ppermute x9, starting transfers between devices, exp_flip(): return lax.ppermute(x, 'exp', [(e, e ^ bit) for e in range(n_exp)])  17.5 us
    ppermute x3, waiting for transfers between devices, gather_prefix_halves(): lax.ppermute(along_x, 'req', req_shift_pairs(n_req, 'y', d))  15.5 us
    dot_general x1, matrix products, body(): jnp.dot(hidden, down_full, preferred_element_type=jnp.float32)  10.2 us
    all_to_all x1, starting transfers between devices, body(): lax.all_to_all(send, 'req', split_axis=0, concat_axis=0, tiled=True)  7.28 us
    ppermute x2, starting transfers between devices, far_relay(): hop = lax.ppermute(x, ('req', 'exp'), first)  6.9 us
  transfers between devices with their start and end apart: 22, of which 13 were waited for; matrix products, arithmetic and copies ran while one was open for 26% of the time, Pallas kernels for 0%

profile of v2, /device:TPU:3, one launch (start us, length us, event | category | flops | bytes accessed | tf_op | source)
XLA Modules:
  0.0 285.7 jit_solution(4453513933464544768)
XLA Ops:
  8.6 3.6 %collective-permute-start.10 = (bf16[384,1536]{1,0:T(8,128)(2,1)}, bf16[384,1536]{1,0:T(8,128)(2,1)}, u32[]{:S(2)}, u32[]{:S(2)}) collective-permute-start(bf16[384,1536]{1,0:T(8,128)(2,1)} %param.19), channel_id=1, source_target_pairs={{0,16},{1,19},{2,18},{3,17},{4,20},{5,23},{6,22},{7,21},{8,24},{9,... | collective-permute-start | bytes 3538952 | tf_op jit(solution)/shard_map/ppermute | solution.py:66
  16.0 2.6 collective-permute-start.5
  22.1 3.3 %collective-permute-start.13 = (bf16[1,576,1536]{2,1,0:T(8,128)(2,1)S(1)}, bf16[1,576,1536]{2,1,0:T(8,128)(2,1)}, u32[]{:S(2)}, u32[]{:S(2)}) collective-permute-start(bf16[1,576,1536]{2,1,0:T(8,128)(2,1)S(1)} %bitcast.129), channel_id=1, source_target_pairs={{0,16},{1,19},{2,18},{3,17},{4,20},{5,23},{6,22},{7,21},{8,24},{9,... | collective-permute-start | bytes 5308424 | tf_op jit(solution)/shard_map/ppermute | solution.py:66
  26.9 12.4 %collective-permute-done.5 = bf16[4,2,128,2,128]{4,2,3,1,0:T(8,128)(2,1)} collective-permute-done((bf16[4,2,128,2,128]{4,2,3,1,0:T(8,128)(2,1)}, bf16[4,2,128,2,128]{4,2,3,1,0:T(8,128)(2,1)}, u32[]{:S(2)}, u32[]{:S(2)}) %collective-permute-start.5) | collective-permute-done | bytes 524320 | tf_op jit(solution)/shard_map/ppermute | solution.py:85
  40.9 3.1 %pad_maximum_fusion.3 = bf16[4,4,2,128,2,128]{5,3,4,2,1,0:T(8,128)(2,1)} fusion(bf16[1,4,2,128,2,128]{5,3,4,2,1,0:T(8,128)(2,1)} %bitcast.16, bf16[1,4,2,128,2,128]{5,3,4,2,1,0:T(8,128)(2,1)} %bitcast.15, bf16[1,4,2,128,2,128]{5,3,4,2,1,0:T(8,128)(2,1)} %bitcast.14, bf16[1,4,2,128,2,128]{5,3,4,2,1,0:T(8,128)(2,1)} %get-tuple-element.18), kind=kLoop, calls=%fused_computation.45 | loop fusion | flops 3145728 | bytes 4194304 | tf_op jit(solution)/shard_map/stack | solution.py:84
  55.2 2.2 fusion.19
  59.7 2.2 gather_fusion.2
  62.3 4.0 %collective-permute-done.11 = bf16[384,1536]{1,0:T(8,128)(2,1)} collective-permute-done((bf16[384,1536]{1,0:T(8,128)(2,1)}, bf16[384,1536]{1,0:T(8,128)(2,1)}, u32[]{:S(2)}, u32[]{:S(2)}) %collective-permute-start.11) | collective-permute-done | bytes 1179680 | tf_op jit(solution)/shard_map/ppermute | solution.py:67
  66.3 3.2 %pad_maximum_fusion.2 = bf16[768,1536]{1,0:T(8,128)(2,1)} fusion(bf16[384,1536]{1,0:T(8,128)(2,1)} %collective-permute-done.11, bf16[384,1536]{1,0:T(8,128)(2,1)} %param.19), kind=kLoop, calls=%fused_computation.44 | loop fusion | flops 4718592 | bytes 4718592 | tf_op jit(solution)/shard_map/concatenate | solution.py:72
  69.5 2.4 collective-permute-start.12
  71.9 3.0 %gather_fusion.1 = bf16[8,128,2,128]{3,1,2,0:T(8,128)(2,1)} fusion(bf16[32,128,2,128]{3,1,2,0:T(8,128)(2,1)} %collective-permute-done.7, s32[1024]{0:T(1024)S(1)} %get-tuple-element.35), kind=kCustom, calls=%fused_computation.1 | custom fusion | bytes 1048608 | tf_op jit(solution)/shard_map/gather | solution.py:155
  77.0 3.0 %gather_fusion.3 = bf16[8,128,2,128]{3,1,2,0:T(8,128)(2,1)} fusion(bf16[32,128,2,128]{3,1,2,0:T(8,128)(2,1)} %collective-permute-done.7, s32[1024]{0:T(1024)S(1)} %get-tuple-element.34), kind=kCustom, calls=%fused_computation.3 | custom fusion | bytes 1048608 | tf_op jit(solution)/shard_map/gather | solution.py:155
  86.6 3.5 %fusion.32 = f32[512,3,256]{2,0,1:T(8,128)S(1)} fusion(f32[2048,512,3]{1,0,2:T(8,128)S(1)} %get-tuple-element.29, f32[3,512]{1,0:T(4,128)S(1)} %add.212, f32[3,512]{1,0:T(4,128)S(1)} %max.14, bf16[2048,128]{1,0:T(8,128)(2,1)S(1)} %copy-done.13, bf16[2048,128]{1,0:T(8,128)(2,1)S(1)} %copy-done.12), kind=kOutput, calls=%fused_computation.57 | convolution fusion | flops 1622147072 | bytes 15216640 | tf_op jit(solution)/shard_map/htp,pd->thd/dot_general | solution.py:182
  93.4 10.3 %collective-permute-done.8 = bf16[512,384]{0,1:T(8,128)(2,1)S(1)} collective-permute-done((bf16[512,384]{0,1:T(8,128)(2,1)S(1)}, bf16[512,384]{0,1:T(8,128)(2,1)S(1)}, u32[]{:S(2)}, u32[]{:S(2)}) %collective-permute-start.8) | collective-permute-done | bytes 393248 | tf_op jit(solution)/shard_map/ppermute | solution.py:43
  104.7 3.7 %pad_maximum_fusion.1 = bf16[2,576,1536]{2,1,0:T(8,128)(2,1)} fusion(bf16[1,576,1536]{2,1,0:T(8,128)(2,1)} %collective-permute-done.14, bf16[1,576,1536]{2,1,0:T(8,128)(2,1)S(1)} %bitcast.130), kind=kLoop, calls=%fused_computation.27 | loop fusion | flops 1769472 | bytes 7077888 | tf_op jit(solution)/shard_map/concatenate | solution.py:72
  110.1 5.5 %fusion.10 = (f32[512]{0:T(512)S(1)}, bf16[512,1536]{1,0:T(8,128)(2,1)S(1)}) fusion(bf16[768,1536]{1,0:T(8,128)(2,1)} %collective-permute-done.12, bf16[384,1536]{1,0:T(8,128)(2,1)} %collective-permute-done.11, bf16[384,1536]{1,0:T(8,128)(2,1)} %param.19, bf16[512,768]{0,1:T(8,128)(2,1)} %collective-permute-done.9, ...), kind=kOutput, calls=%fused_computation.28 | convolution fusion | flops 2439511552 | bytes 9439232 | tf_op jit(solution)/shard_map/dot_general | solution.py:190
  115.7 3.8 %convolution_convert_fusion.1 = bf16[1024,1536]{1,0:T(8,128)(2,1)} fusion(pred[512,1024]{1,0:T(8,128)(4,1)S(1)} %fusion.2, bf16[512,1536]{1,0:T(8,128)(2,1)S(1)} %get-tuple-element.33, f32[1536]{0:T(1024)S(1)} %copy-done.20, f32[512]{0:T(512)S(1)} %add_rsqrt_fusion), kind=kOutput, calls=%fused_computation.26 | convolution fusion | flops 1615331328 | bytes 5251072 | tf_op jit(solution)/shard_map/tq,td->qd/dot_general | solution.py:209
  119.5 7.3 %all-to-all-start = ((bf16[32,32,1536]{2,1,0:T(8,128)(2,1)}), bf16[32,32,1536]{2,1,0:T(8,128)(2,1)}, u32[]{:S(2)}, u32[]{:S(2)}) async-start(bf16[32,32,1536]{2,1,0:T(8,128)(2,1)} %bitcast.134), calls=%async_computation | async-start | bytes 6291456 | tf_op jit(solution)/shard_map/all_to_all | solution.py:211
  126.8 3.4 %pad_maximum_fusion = bf16[4,576,1536]{2,1,0:T(8,128)(2,1)S(1)} fusion(bf16[2,576,1536]{2,1,0:T(8,128)(2,1)} %collective-permute-done.15, bf16[1,576,1536]{2,1,0:T(8,128)(2,1)} %collective-permute-done.14, bf16[1,576,1536]{2,1,0:T(8,128)(2,1)S(1)} %bitcast.131), kind=kLoop, calls=%fused_computation.12 | loop fusion | flops 7077888 | bytes 14155776 | tf_op jit(solution)/shard_map/concatenate | solution.py:73
  130.2 2.6 fusion.89
  132.8 36.2 %all-to-all-done = bf16[32,32,1536]{2,1,0:T(8,128)(2,1)} async-done(((bf16[32,32,1536]{2,1,0:T(8,128)(2,1)}), bf16[32,32,1536]{2,1,0:T(8,128)(2,1)}, u32[]{:S(2)}, u32[]{:S(2)}) %all-to-all-start) | async-done | bytes 3145760 | tf_op jit(solution)/shard_map/all_to_all | solution.py:211
  169.0 6.9 %fusion.91 = f32[1024,768]{1,0:T(8,128)} fusion(bf16[1024,1536]{1,0:T(8,128)(2,1)} %bitcast.40, bf16[768,1536]{1,0:T(8,128)(2,1)} %bitcast.138), kind=kOutput, calls=%fused_computation.198 | convolution fusion | flops 2415919104 | bytes 8650752 | tf_op jit(solution)/shard_map/dot_general | solution.py:213
  175.9 10.2 %convolution_convert_fusion = bf16[1024,1536]{1,0:T(8,128)(2,1)} fusion(bf16[768,1536]{1,0:T(8,128)(2,1)} %bitcast.137, f32[1024,768]{1,0:T(8,128)} %fusion.91, bf16[1024,1536]{1,0:T(8,128)(2,1)} %bitcast.40, bf16[768,1536]{1,0:T(8,128)(2,1)S(1)} %bitcast.136), kind=kOutput, calls=%fused_computation.25 | convolution fusion | flops 4835770368 | bytes 14155776 | tf_op jit(solution)/shard_map/dot_general | solution.py:216
  186.1 5.0 %all-to-all-start.1 = ((bf16[32,32,1536]{2,1,0:T(8,128)(2,1)}), bf16[32,32,1536]{2,1,0:T(8,128)(2,1)S(1)}, u32[]{:S(2)}, u32[]{:S(2)}) async-start(bf16[32,32,1536]{2,1,0:T(8,128)(2,1)} %bitcast.135), calls=%async_computation.1 | async-start | bytes 6291456 | tf_op jit(solution)/shard_map/all_to_all | solution.py:218
  191.1 2.7 select_reduce_fusion
  193.8 39.8 %all-to-all-done.1 = bf16[32,32,1536]{2,1,0:T(8,128)(2,1)S(1)} async-done(((bf16[32,32,1536]{2,1,0:T(8,128)(2,1)}), bf16[32,32,1536]{2,1,0:T(8,128)(2,1)S(1)}, u32[]{:S(2)}, u32[]{:S(2)}) %all-to-all-start.1) | async-done | bytes 3145760 | tf_op jit(solution)/shard_map/all_to_all | solution.py:218
  233.6 2.3 fusion.53
  243.7 2.8 dynamic-slice_add_fusion
  246.5 3.5 %collective-permute-start.17 = (f32[128,1536]{1,0:T(8,128)}, f32[128,1536]{1,0:T(8,128)}, u32[]{:S(2)}, u32[]{:S(2)}) collective-permute-start(f32[128,1536]{1,0:T(8,128)} %dynamic-slice_add_fusion), channel_id=1, source_target_pairs={{0,2},{1,3},{2,0},{3,1},{4,6},{5,7},{6,4},{7,5},{8,10},{9,11},{10,... | collective-permute-start | bytes 2359304 | tf_op jit(solution)/shard_map/ppermute | solution.py:43
  253.3 14.6 %collective-permute-done.17 = f32[128,1536]{1,0:T(8,128)} collective-permute-done((f32[128,1536]{1,0:T(8,128)}, f32[128,1536]{1,0:T(8,128)}, u32[]{:S(2)}, u32[]{:S(2)}) %collective-permute-start.17) | collective-permute-done | bytes 786464 | tf_op jit(solution)/shard_map/ppermute | solution.py:43
  269.7 2.8 collective-permute-start.18
  272.4 8.5 %collective-permute-done.18 = bf16[128,1536]{1,0:T(8,128)(2,1)S(1)} collective-permute-done((bf16[128,1536]{1,0:T(8,128)(2,1)S(1)}, bf16[128,1536]{1,0:T(8,128)(2,1)S(1)}, u32[]{:S(2)}, u32[]{:S(2)}) %collective-permute-start.18) | collective-permute-done | bytes 393248 | tf_op jit(solution)/shard_map/ppermute | solution.py:43
  (125 shorter events, 63.3 us)
Async XLA Ops:
  0.0 50.0 %copy-start = (bf16[1536,2,256]{2,1,0:T(2,128)(2,1)S(1)}, bf16[1536,2,256]{2,1,0:T(2,128)(2,1)}, u32[]{:S(2)}) copy-start(bf16[1536,2,256]{2,1,0:T(2,128)(2,1)} %param.18) | copy-start | bytes 4718596
  0.0 12.2 %copy-start.21 = (s32[64]{0:T(128)S(1)}, s32[64]{0:T(128)}, u32[]{:S(2)}) copy-start(s32[64]{0:T(128)} %param.22) | copy-start | bytes 772
  1.2 3.4 %collective-permute-start = (bf16[128,2,128]{2,0,1:T(8,128)(2,1)S(1)}, bf16[128,2,128]{2,0,1:T(8,128)(2,1)S(1)}, u32[]{:S(2)}, u32[]{:S(2)}) collective-permute-start(bf16[128,2,128]{2,0,1:T(8,128)(2,1)S(1)} %bitcast.148), channel_id=1, source_target_pairs={{0,16},{4,20},{8,24},{12,28},{16,0},{20,4},{24,8},{28,12},{32,48},... | collective-permute-start | bytes 196616 | tf_op jit(solution)/shard_map/ppermute | solution.py:77
  4.5 17.6 %copy-start.22 = (s32[64]{0:T(128)S(1)}, s32[64]{0:T(128)}, u32[]{:S(2)}) copy-start(s32[64]{0:T(128)} %param.21) | copy-start | bytes 772
  4.6 7.6 %collective-permute-start.1 = (bf16[2,128,2,128]{3,1,2,0:T(8,128)(2,1)S(1)}, bf16[2,128,2,128]{3,1,2,0:T(8,128)(2,1)}, u32[]{:S(2)}, u32[]{:S(2)}) collective-permute-start(bf16[2,128,2,128]{3,1,2,0:T(8,128)(2,1)S(1)} %pad_maximum_fusion.9), channel_id=1, source_target_pairs={{0,4},{4,8},{8,12},{12,0},{16,20},{20,24},{24,28},{28,16},{32,36},... | collective-permute-start | bytes 393224 | tf_op jit(solution)/shard_map/ppermute | solution.py:82
  5.9 6.4 %collective-permute-start.2 = (bf16[2,128,2,128]{3,1,2,0:T(8,128)(2,1)S(1)}, bf16[2,128,2,128]{3,1,2,0:T(8,128)(2,1)}, u32[]{:S(2)}, u32[]{:S(2)}) collective-permute-start(bf16[2,128,2,128]{3,1,2,0:T(8,128)(2,1)S(1)} %pad_maximum_fusion.9), channel_id=1, source_target_pairs={{0,8},{4,12},{8,0},{12,4},{16,24},{20,28},{24,16},{28,20},{32,40},... | collective-permute-start | bytes 393224 | tf_op jit(solution)/shard_map/ppermute | solution.py:82
  6.7 5.9 %collective-permute-start.3 = (bf16[2,128,2,128]{3,1,2,0:T(8,128)(2,1)S(1)}, bf16[2,128,2,128]{3,1,2,0:T(8,128)(2,1)}, u32[]{:S(2)}, u32[]{:S(2)}) collective-permute-start(bf16[2,128,2,128]{3,1,2,0:T(8,128)(2,1)S(1)} %pad_maximum_fusion.9), channel_id=1, source_target_pairs={{0,12},{4,0},{8,4},{12,8},{16,28},{20,16},{24,20},{28,24},{32,44},... | collective-permute-start | bytes 393224 | tf_op jit(solution)/shard_map/ppermute | solution.py:82
  8.6 42.0 %collective-permute-start.10 = (bf16[384,1536]{1,0:T(8,128)(2,1)}, bf16[384,1536]{1,0:T(8,128)(2,1)}, u32[]{:S(2)}, u32[]{:S(2)}) collective-permute-start(bf16[384,1536]{1,0:T(8,128)(2,1)} %param.19), channel_id=1, source_target_pairs={{0,16},{1,19},{2,18},{3,17},{4,20},{5,23},{6,22},{7,21},{8,24},{9,... | collective-permute-start | bytes 3538952 | tf_op jit(solution)/shard_map/ppermute | solution.py:66
  12.2 7.5 %copy-start.4 = (bf16[512,1536]{1,0:T(8,128)(2,1)S(1)}, bf16[512,1536]{1,0:T(8,128)(2,1)}, u32[]{:S(2)}) copy-start(bf16[512,1536]{1,0:T(8,128)(2,1)} %param.15) | copy-start | bytes 4718596
  14.7 12.2 %collective-permute-start.4 = (bf16[4,2,128,2,128]{4,2,3,1,0:T(8,128)(2,1)}, bf16[4,2,128,2,128]{4,2,3,1,0:T(8,128)(2,1)}, u32[]{:S(2)}, u32[]{:S(2)}) collective-permute-start(bf16[4,2,128,2,128]{4,2,3,1,0:T(8,128)(2,1)} %get-tuple-element.19), channel_id=1, source_target_pairs={{0,32},{4,36},{8,40},{12,44},{16,48},{20,52},{24,56},{28,60},{32,6... | collective-permute-start | bytes 1572872 | tf_op jit(solution)/shard_map/ppermute | solution.py:85
  16.0 23.3 %collective-permute-start.5 = (bf16[4,2,128,2,128]{4,2,3,1,0:T(8,128)(2,1)}, bf16[4,2,128,2,128]{4,2,3,1,0:T(8,128)(2,1)}, u32[]{:S(2)}, u32[]{:S(2)}) collective-permute-start(bf16[4,2,128,2,128]{4,2,3,1,0:T(8,128)(2,1)} %get-tuple-element.19), channel_id=1, source_target_pairs={{0,64},{4,68},{8,72},{12,76},{16,80},{20,84},{24,88},{28,92},{32,9... | collective-permute-start | bytes 1572872 | tf_op jit(solution)/shard_map/ppermute | solution.py:85
  18.6 22.3 %collective-permute-start.6 = (bf16[4,2,128,2,128]{4,2,3,1,0:T(8,128)(2,1)}, bf16[4,2,128,2,128]{4,2,3,1,0:T(8,128)(2,1)}, u32[]{:S(2)}, u32[]{:S(2)}) collective-permute-start(bf16[4,2,128,2,128]{4,2,3,1,0:T(8,128)(2,1)} %get-tuple-element.19), channel_id=1, source_target_pairs={{0,96},{4,100},{8,104},{12,108},{16,112},{20,116},{24,120},{28,124... | collective-permute-start | bytes 1572872 | tf_op jit(solution)/shard_map/ppermute | solution.py:85
  20.1 26.1 %copy-start.19 = (f32[1536]{0:T(1024)S(1)}, f32[1536]{0:T(1024)}, u32[]{:S(2)}) copy-start(f32[1536]{0:T(1024)} %param.16) | copy-start | bytes 18436
  22.0 24.2 %copy-start.5 = (bf16[512,1536]{1,0:T(8,128)(2,1)S(1)}, bf16[512,1536]{1,0:T(8,128)(2,1)}, u32[]{:S(2)}) copy-start(bf16[512,1536]{1,0:T(8,128)(2,1)} %param.15) | copy-start | bytes 4718596
  22.0 24.2 %copy-start.18 = (bf16[1536,384]{1,0:T(8,128)(2,1)S(1)}, bf16[1536,384]{1,0:T(8,128)(2,1)}, u32[]{:S(2)}) copy-start(bf16[1536,384]{1,0:T(8,128)(2,1)} %param.17) | copy-start | bytes 3538948
  22.1 39.8 %collective-permute-start.13 = (bf16[1,576,1536]{2,1,0:T(8,128)(2,1)S(1)}, bf16[1,576,1536]{2,1,0:T(8,128)(2,1)}, u32[]{:S(2)}, u32[]{:S(2)}) collective-permute-start(bf16[1,576,1536]{2,1,0:T(8,128)(2,1)S(1)} %bitcast.129), channel_id=1, source_target_pairs={{0,16},{1,19},{2,18},{3,17},{4,20},{5,23},{6,22},{7,21},{8,24},{9,... | collective-permute-start | bytes 5308424 | tf_op jit(solution)/shard_map/ppermute | solution.py:66
  44.1 5.8 %copy-start.17 = (s32[32]{0:T(128)S(1)}, s32[32]{0:T(128)}, u32[]{:S(2)}) copy-start(s32[32]{0:T(128)} %param.23) | copy-start | bytes 388
  44.1 27.9 %collective-permute-start.7 = (bf16[32,128,2,128]{3,1,2,0:T(8,128)(2,1)}, bf16[32,128,2,128]{3,1,2,0:T(8,128)(2,1)}, u32[]{:S(2)}, u32[]{:S(2)}) collective-permute-start(bf16[32,128,2,128]{3,1,2,0:T(8,128)(2,1)} %bitcast.17), channel_id=1, source_target_pairs={{0,1},{1,0},{2,3},{3,2},{4,5},{5,4},{6,7},{7,6},{8,9},{9,8},{10,11... | collective-permute-start | bytes 6291464 | tf_op jit(solution)/shard_map/ppermute | solution.py:43
  50.6 15.7 %collective-permute-start.11 = (bf16[384,1536]{1,0:T(8,128)(2,1)}, bf16[384,1536]{1,0:T(8,128)(2,1)}, u32[]{:S(2)}, u32[]{:S(2)}) collective-permute-start(bf16[384,1536]{1,0:T(8,128)(2,1)} %collective-permute-done.10), channel_id=1, source_target_pairs={{0,18},{1,17},{2,16},{3,19},{4,22},{5,21},{6,20},{7,23},{8,26},{9,... | collective-permute-start | bytes 3538952 | tf_op jit(solution)/shard_map/ppermute | solution.py:67
  61.9 42.8 %collective-permute-start.14 = (bf16[1,576,1536]{2,1,0:T(8,128)(2,1)}, bf16[1,576,1536]{2,1,0:T(8,128)(2,1)}, u32[]{:S(2)}, u32[]{:S(2)}) collective-permute-start(bf16[1,576,1536]{2,1,0:T(8,128)(2,1)} %collective-permute-done.13), channel_id=1, source_target_pairs={{0,18},{1,17},{2,16},{3,19},{4,22},{5,21},{6,20},{7,23},{8,26},{9,... | collective-permute-start | bytes 5308424 | tf_op jit(solution)/shard_map/ppermute | solution.py:67
  69.5 40.6 %collective-permute-start.12 = (bf16[768,1536]{1,0:T(8,128)(2,1)}, bf16[768,1536]{1,0:T(8,128)(2,1)}, u32[]{:S(2)}, u32[]{:S(2)}) collective-permute-start(bf16[768,1536]{1,0:T(8,128)(2,1)} %pad_maximum_fusion.2), channel_id=1, source_target_pairs={{0,1},{1,0},{2,3},{3,2},{4,5},{5,4},{6,7},{7,6},{8,9},{9,8},{10,11... | collective-permute-start | bytes 7077896 | tf_op jit(solution)/shard_map/ppermute | solution.py:43
  91.4 12.3 %collective-permute-start.8 = (bf16[512,384]{0,1:T(8,128)(2,1)S(1)}, bf16[512,384]{0,1:T(8,128)(2,1)S(1)}, u32[]{:S(2)}, u32[]{:S(2)}) collective-permute-start(bf16[512,384]{0,1:T(8,128)(2,1)S(1)} %bitcast.139), channel_id=1, source_target_pairs={{0,2},{1,3},{2,0},{3,1},{4,6},{5,7},{6,4},{7,5},{8,10},{9,11},{10,... | collective-permute-start | bytes 1179656 | tf_op jit(solution)/shard_map/ppermute | solution.py:43
  103.7 6.4 %collective-permute-start.9 = (bf16[512,768]{0,1:T(8,128)(2,1)S(1)}, bf16[512,768]{0,1:T(8,128)(2,1)}, u32[]{:S(2)}, u32[]{:S(2)}) collective-permute-start(bf16[512,768]{0,1:T(8,128)(2,1)S(1)} %pad_maximum_fusion.7), channel_id=1, source_target_pairs={{0,1},{1,0},{2,3},{3,2},{4,5},{5,4},{6,7},{7,6},{8,9},{9,8},{10,11... | collective-permute-start | bytes 2359304 | tf_op jit(solution)/shard_map/ppermute | solution.py:43
  104.7 5.4 %copy-start.7 = (bf16[512,1536]{1,0:T(8,128)(2,1)S(1)}, bf16[512,1536]{1,0:T(8,128)(2,1)}, u32[]{:S(2)}) copy-start(bf16[512,1536]{1,0:T(8,128)(2,1)} %param.15) | copy-start | bytes 4718596
  108.5 18.3 %collective-permute-start.15 = (bf16[2,576,1536]{2,1,0:T(8,128)(2,1)}, bf16[2,576,1536]{2,1,0:T(8,128)(2,1)}, u32[]{:S(2)}, u32[]{:S(2)}) collective-permute-start(bf16[2,576,1536]{2,1,0:T(8,128)(2,1)} %pad_maximum_fusion.1), channel_id=1, source_target_pairs={{0,1},{1,0},{2,3},{3,2},{4,5},{5,4},{6,7},{7,6},{8,9},{9,8},{10,11... | collective-permute-start | bytes 10616840 | tf_op jit(solution)/shard_map/ppermute | solution.py:43
  110.1 5.6 %copy-start.20 = (f32[1536]{0:T(1024)S(1)}, f32[1536]{0:T(1024)}, u32[]{:S(2)}) copy-start(f32[1536]{0:T(1024)} %param.24) | copy-start | bytes 18436
  119.5 49.6 %all-to-all-start = ((bf16[32,32,1536]{2,1,0:T(8,128)(2,1)}), bf16[32,32,1536]{2,1,0:T(8,128)(2,1)}, u32[]{:S(2)}, u32[]{:S(2)}) async-start(bf16[32,32,1536]{2,1,0:T(8,128)(2,1)} %bitcast.134), calls=%async_computation | async-start | bytes 6291456 | tf_op jit(solution)/shard_map/all_to_all | solution.py:211
  186.1 47.5 %all-to-all-start.1 = ((bf16[32,32,1536]{2,1,0:T(8,128)(2,1)}), bf16[32,32,1536]{2,1,0:T(8,128)(2,1)S(1)}, u32[]{:S(2)}, u32[]{:S(2)}) async-start(bf16[32,32,1536]{2,1,0:T(8,128)(2,1)} %bitcast.135), calls=%async_computation.1 | async-start | bytes 6291456 | tf_op jit(solution)/shard_map/all_to_all | solution.py:218
  238.1 5.5 %collective-permute-start.16 = (f32[256,1536]{1,0:T(8,128)}, f32[256,1536]{1,0:T(8,128)}, u32[]{:S(2)}, u32[]{:S(2)}) collective-permute-start(f32[256,1536]{1,0:T(8,128)} %convolution_add_fusion), channel_id=1, source_target_pairs={{0,1},{1,0},{2,3},{3,2},{4,5},{5,4},{6,7},{7,6},{8,9},{9,8},{10,11... | collective-permute-start | bytes 4718600 | tf_op jit(solution)/shard_map/ppermute | solution.py:43
  246.5 21.4 %collective-permute-start.17 = (f32[128,1536]{1,0:T(8,128)}, f32[128,1536]{1,0:T(8,128)}, u32[]{:S(2)}, u32[]{:S(2)}) collective-permute-start(f32[128,1536]{1,0:T(8,128)} %dynamic-slice_add_fusion), channel_id=1, source_target_pairs={{0,2},{1,3},{2,0},{3,1},{4,6},{5,7},{6,4},{7,5},{8,10},{9,11},{10,... | collective-permute-start | bytes 2359304 | tf_op jit(solution)/shard_map/ppermute | solution.py:43
  269.7 11.3 %collective-permute-start.18 = (bf16[128,1536]{1,0:T(8,128)(2,1)S(1)}, bf16[128,1536]{1,0:T(8,128)(2,1)S(1)}, u32[]{:S(2)}, u32[]{:S(2)}) collective-permute-start(bf16[128,1536]{1,0:T(8,128)(2,1)S(1)} %get-tuple-element.10), channel_id=1, source_target_pairs={{0,2},{1,3},{2,0},{3,1},{4,6},{5,7},{6,4},{7,5},{8,10},{9,11},{10,... | collective-permute-start | bytes 1179656 | tf_op jit(solution)/shard_map/ppermute | solution.py:43
  281.0 3.8 %collective-permute-start.19 = (bf16[256,1536]{1,0:T(8,128)(2,1)S(1)}, bf16[256,1536]{1,0:T(8,128)(2,1)S(1)}, u32[]{:S(2)}, u32[]{:S(2)}) collective-permute-start(bf16[256,1536]{1,0:T(8,128)(2,1)S(1)} %constant_dynamic-update-slice_fusion.2), channel_id=1, source_target_pairs={{0,1},{1,0},{2,3},{3,2},{4,5},{5,4},{6,7},{7,6},{8,9},{9,8},{10,11... | collective-permute-start | bytes 2359304 | tf_op jit(solution)/shard_map/ppermute | solution.py:43
  (13 other events, 31.6 us)

commit v3 on v2

--- a/solution.py
+++ b/solution.py
@@ -121,7 +121,7 @@
     along_z = gather_prefix_near(mine, n_req)
     ff_shard = w_gate.shape[2]
     packed = jnp.concatenate([w_gate[0].T, w_up[0].T, w_down[0]], axis=0)
-    packed_late, along_z = lax.optimization_barrier((packed, along_z))
+    packed_late = packed
     w_output_late = w_output
     halves_mine = gather_prefix_halves(along_z, n_req)
     halves_other = exp_flip(halves_mine, n_exp, 1)

time: 287 us -> 288 us (level)
  starting transfers between devices: 49 us -> 42.9 us
  waiting for transfers between devices: 133 us -> 138 us
    ppermute x3, waiting for transfers between devices: 15.5 us -> 20 us  [gather_prefix_halves(): lax.ppermute(along_x, 'req', req_shift_pairs(n_req, 'y', d))]
    ppermute x9, starting transfers between devices: 17.5 us -> 14.3 us  [exp_flip(): return lax.ppermute(x, 'exp', [(e, e ^ bit) for e in range(n_exp)])]
  transfers between devices with their start and end apart: 22 -> 22, of which waited for: 13 -> 12; matrix products, arithmetic and copies ran while one was open for 26% -> 26% of each run, Pallas kernels for 0% -> 0%
where the time goes in v3:
time: 288 us; the launch traced here: 287 us
  waiting for transfers between devices  138 us (48%)
  matrix products  49.5 us (17%)
  starting transfers between devices  42.9 us (15%)
  other arithmetic  32.2 us (11%)
  local copies, waits for them, and re-layouts  21.6 us (8%)
    all_to_all x1, waiting for transfers between devices, body(): back = lax.all_to_all(part, 'req', split_axis=0, concat_axis=0, tiled=True)  39.6 us
    ppermute x9, waiting for transfers between devices, exp_flip(): return lax.ppermute(x, 'exp', [(e, e ^ bit) for e in range(n_exp)])  37.8 us
    all_to_all x1, waiting for transfers between devices, body(): lax.all_to_all(send, 'req', split_axis=0, concat_axis=0, tiled=True)  36.2 us
    ppermute x3, waiting for transfers between devices, gather_prefix_halves(): lax.ppermute(along_x, 'req', req_shift_pairs(n_req, 'y', d))  20 us
    ppermute x9, starting transfers between devices, exp_flip(): return lax.ppermute(x, 'exp', [(e, e ^ bit) for e in range(n_exp)])  14.3 us
    dot_general x1, matrix products, body(): jnp.dot(hidden, down_full, preferred_element_type=jnp.float32)  10.2 us
    concatenate x2, other arithmetic, gather_exp_relay(): near = exp_flip(jnp.concatenate([x, far], axis=axis), n_exp, 1)  6.93 us
    dot_general x1, matrix products, body(): gate = jnp.dot(rows, gate_full, preferred_element_type=jnp.float32)  6.88 us
  transfers between devices with their start and end apart: 22, of which 12 were waited for; matrix products, arithmetic and copies ran while one was open for 26% of the time, Pallas kernels for 0%

profile of v3, /device:TPU:3, one launch (start us, length us, event | category | flops | bytes accessed | tf_op | source)
XLA Modules:
  0.0 286.6 jit_solution(9133579411233448789)
XLA Ops:
  2.9 2.2 collective-permute-start.10
  11.3 3.1 %collective-permute-start.13 = (bf16[1,576,1536]{2,1,0:T(8,128)(2,1)S(1)}, bf16[1,576,1536]{2,1,0:T(8,128)(2,1)}, u32[]{:S(2)}, u32[]{:S(2)}) collective-permute-start(bf16[1,576,1536]{2,1,0:T(8,128)(2,1)S(1)} %maximum_bitcast_fusion), channel_id=1, source_target_pairs={{0,16},{1,19},{2,18},{3,17},{4,20},{5,23},{6,22},{7,21},{8,24},{9,... | collective-permute-start | bytes 5308424 | tf_op jit(solution)/shard_map/ppermute | solution.py:66
  17.4 2.9 %collective-permute-start.5 = (bf16[4,2,128,2,128]{4,2,3,1,0:T(8,128)(2,1)}, bf16[4,2,128,2,128]{4,2,3,1,0:T(8,128)(2,1)}, u32[]{:S(2)}, u32[]{:S(2)}) collective-permute-start(bf16[4,2,128,2,128]{4,2,3,1,0:T(8,128)(2,1)} %get-tuple-element.15), channel_id=1, source_target_pairs={{0,64},{4,68},{8,72},{12,76},{16,80},{20,84},{24,88},{28,92},{32,9... | collective-permute-start | bytes 1572872 | tf_op jit(solution)/shard_map/ppermute | solution.py:85
  24.3 6.8 %collective-permute-done.5 = bf16[4,2,128,2,128]{4,2,3,1,0:T(8,128)(2,1)} collective-permute-done((bf16[4,2,128,2,128]{4,2,3,1,0:T(8,128)(2,1)}, bf16[4,2,128,2,128]{4,2,3,1,0:T(8,128)(2,1)}, u32[]{:S(2)}, u32[]{:S(2)}) %collective-permute-start.5) | collective-permute-done | bytes 524320 | tf_op jit(solution)/shard_map/ppermute | solution.py:85
  31.1 12.5 %collective-permute-done.6 = bf16[4,2,128,2,128]{4,2,3,1,0:T(8,128)(2,1)} collective-permute-done((bf16[4,2,128,2,128]{4,2,3,1,0:T(8,128)(2,1)}, bf16[4,2,128,2,128]{4,2,3,1,0:T(8,128)(2,1)}, u32[]{:S(2)}, u32[]{:S(2)}) %collective-permute-start.6) | collective-permute-done | bytes 524320 | tf_op jit(solution)/shard_map/ppermute | solution.py:85
  44.3 3.1 %pad_maximum_fusion.3 = bf16[4,4,2,128,2,128]{5,3,4,2,1,0:T(8,128)(2,1)} fusion(bf16[1,4,2,128,2,128]{5,3,4,2,1,0:T(8,128)(2,1)} %bitcast.11, bf16[1,4,2,128,2,128]{5,3,4,2,1,0:T(8,128)(2,1)} %bitcast.10, bf16[1,4,2,128,2,128]{5,3,4,2,1,0:T(8,128)(2,1)} %bitcast.9, bf16[1,4,2,128,2,128]{5,3,4,2,1,0:T(8,128)(2,1)} %get-tuple-element.14), kind=kLoop, calls=%fused_computation.45 | loop fusion | flops 3145728 | bytes 4194304 | tf_op jit(solution)/shard_map/stack | solution.py:84
  56.1 2.2 fusion.19
  64.3 4.1 %collective-permute-done.11 = bf16[384,1536]{1,0:T(8,128)(2,1)} collective-permute-done((bf16[384,1536]{1,0:T(8,128)(2,1)}, bf16[384,1536]{1,0:T(8,128)(2,1)}, u32[]{:S(2)}, u32[]{:S(2)}) %collective-permute-start.11) | collective-permute-done | bytes 1179680 | tf_op jit(solution)/shard_map/ppermute | solution.py:67
  68.4 3.2 %pad_maximum_fusion.2 = bf16[768,1536]{1,0:T(8,128)(2,1)} fusion(bf16[384,1536]{1,0:T(8,128)(2,1)} %collective-permute-done.11, bf16[384,1536]{1,0:T(8,128)(2,1)} %param.19), kind=kLoop, calls=%fused_computation.44 | loop fusion | flops 4718592 | bytes 4718592 | tf_op jit(solution)/shard_map/concatenate | solution.py:72
  73.7 3.0 %gather_fusion.1 = bf16[8,128,2,128]{3,1,2,0:T(8,128)(2,1)} fusion(bf16[32,128,2,128]{3,1,2,0:T(8,128)(2,1)} %collective-permute-done.7, s32[1024]{0:T(1024)S(1)} %get-tuple-element.33), kind=kCustom, calls=%fused_computation.1 | custom fusion | bytes 1048608 | tf_op jit(solution)/shard_map/gather | solution.py:155
  78.8 3.0 %gather_fusion.3 = bf16[8,128,2,128]{3,1,2,0:T(8,128)(2,1)} fusion(bf16[32,128,2,128]{3,1,2,0:T(8,128)(2,1)} %collective-permute-done.7, s32[1024]{0:T(1024)S(1)} %get-tuple-element.32), kind=kCustom, calls=%fused_computation.3 | custom fusion | bytes 1048608 | tf_op jit(solution)/shard_map/gather | solution.py:155
  88.4 3.5 %fusion.32 = f32[512,3,256]{2,0,1:T(8,128)S(1)} fusion(f32[2048,512,3]{1,0,2:T(8,128)S(1)} %get-tuple-element.27, f32[3,512]{1,0:T(4,128)S(1)} %add.212, f32[3,512]{1,0:T(4,128)S(1)} %max.14, bf16[2048,128]{1,0:T(8,128)(2,1)S(1)} %copy-done.14, bf16[2048,128]{1,0:T(8,128)(2,1)S(1)} %copy-done.13), kind=kOutput, calls=%fused_computation.57 | convolution fusion | flops 1622147072 | bytes 15216640 | tf_op jit(solution)/shard_map/htp,pd->thd/dot_general | solution.py:182
  93.6 11.8 %collective-permute-done.8 = bf16[512,384]{0,1:T(8,128)(2,1)S(1)} collective-permute-done((bf16[512,384]{0,1:T(8,128)(2,1)S(1)}, bf16[512,384]{0,1:T(8,128)(2,1)S(1)}, u32[]{:S(2)}, u32[]{:S(2)}) %collective-permute-start.8) | collective-permute-done | bytes 393248 | tf_op jit(solution)/shard_map/ppermute | solution.py:43
  107.4 3.8 %pad_maximum_fusion.1 = bf16[2,576,1536]{2,1,0:T(8,128)(2,1)} fusion(bf16[1,576,1536]{2,1,0:T(8,128)(2,1)} %collective-permute-done.14, bf16[1,576,1536]{2,1,0:T(8,128)(2,1)S(1)} %maximum_bitcast_fusion), kind=kLoop, calls=%fused_computation.27 | loop fusion | flops 1769472 | bytes 7077888 | tf_op jit(solution)/shard_map/concatenate | solution.py:72
  112.9 5.2 %fusion.10 = (f32[512]{0:T(512)S(1)}, bf16[512,1536]{1,0:T(8,128)(2,1)S(1)}) fusion(bf16[768,1536]{1,0:T(8,128)(2,1)} %collective-permute-done.12, bf16[384,1536]{1,0:T(8,128)(2,1)} %collective-permute-done.11, bf16[384,1536]{1,0:T(8,128)(2,1)S(1)} %copy-done.12, bf16[512,768]{0,1:T(8,128)(2,1)} %collective-permute-done.9, ...), kind=kOutput, calls=%fused_computation.28 | convolution fusion | flops 2439511552 | bytes 9439232 | tf_op jit(solution)/shard_map/dot_general | solution.py:190
  118.1 3.8 %convolution_convert_fusion.1 = bf16[1024,1536]{1,0:T(8,128)(2,1)} fusion(pred[512,1024]{1,0:T(8,128)(4,1)S(1)} %fusion.2, bf16[512,1536]{1,0:T(8,128)(2,1)S(1)} %get-tuple-element.31, f32[1536]{0:T(1024)S(1)} %copy-done.23, f32[512]{0:T(512)S(1)} %add_rsqrt_fusion), kind=kOutput, calls=%fused_computation.26 | convolution fusion | flops 1615331328 | bytes 5251072 | tf_op jit(solution)/shard_map/tq,td->qd/dot_general | solution.py:209
  121.8 6.7 %all-to-all-start = ((bf16[32,32,1536]{2,1,0:T(8,128)(2,1)}), bf16[32,32,1536]{2,1,0:T(8,128)(2,1)}, u32[]{:S(2)}, u32[]{:S(2)}) async-start(bf16[32,32,1536]{2,1,0:T(8,128)(2,1)} %bitcast.133), calls=%async_computation | async-start | bytes 6291456 | tf_op jit(solution)/shard_map/all_to_all | solution.py:211
  128.6 3.4 %pad_maximum_fusion = bf16[4,576,1536]{2,1,0:T(8,128)(2,1)S(1)} fusion(bf16[2,576,1536]{2,1,0:T(8,128)(2,1)} %collective-permute-done.15, bf16[1,576,1536]{2,1,0:T(8,128)(2,1)} %collective-permute-done.14, bf16[1,576,1536]{2,1,0:T(8,128)(2,1)S(1)} %maximum_bitcast_fusion), kind=kLoop, calls=%fused_computation.12 | loop fusion | flops 7077888 | bytes 14155776 | tf_op jit(solution)/shard_map/concatenate | solution.py:73
  132.0 2.6 fusion.90
  134.6 36.2 %all-to-all-done = bf16[32,32,1536]{2,1,0:T(8,128)(2,1)} async-done(((bf16[32,32,1536]{2,1,0:T(8,128)(2,1)}), bf16[32,32,1536]{2,1,0:T(8,128)(2,1)}, u32[]{:S(2)}, u32[]{:S(2)}) %all-to-all-start) | async-done | bytes 3145760 | tf_op jit(solution)/shard_map/all_to_all | solution.py:211
  170.8 6.9 %fusion.92 = f32[1024,768]{1,0:T(8,128)} fusion(bf16[1024,1536]{1,0:T(8,128)(2,1)} %bitcast.35, bf16[768,1536]{1,0:T(8,128)(2,1)} %bitcast.137), kind=kOutput, calls=%fused_computation.199 | convolution fusion | flops 2415919104 | bytes 8650752 | tf_op jit(solution)/shard_map/dot_general | solution.py:213
  177.7 10.2 %convolution_convert_fusion = bf16[1024,1536]{1,0:T(8,128)(2,1)} fusion(bf16[768,1536]{1,0:T(8,128)(2,1)} %bitcast.136, f32[1024,768]{1,0:T(8,128)} %fusion.92, bf16[1024,1536]{1,0:T(8,128)(2,1)} %bitcast.35, bf16[768,1536]{1,0:T(8,128)(2,1)S(1)} %bitcast.135), kind=kOutput, calls=%fused_computation.25 | convolution fusion | flops 4835770368 | bytes 14155776 | tf_op jit(solution)/shard_map/dot_general | solution.py:216
  187.9 5.0 %all-to-all-start.1 = ((bf16[32,32,1536]{2,1,0:T(8,128)(2,1)}), bf16[32,32,1536]{2,1,0:T(8,128)(2,1)S(1)}, u32[]{:S(2)}, u32[]{:S(2)}) async-start(bf16[32,32,1536]{2,1,0:T(8,128)(2,1)} %bitcast.134), calls=%async_computation.1 | async-start | bytes 6291456 | tf_op jit(solution)/shard_map/all_to_all | solution.py:218
  192.9 2.7 select_reduce_fusion
  195.6 39.6 %all-to-all-done.1 = bf16[32,32,1536]{2,1,0:T(8,128)(2,1)S(1)} async-done(((bf16[32,32,1536]{2,1,0:T(8,128)(2,1)}), bf16[32,32,1536]{2,1,0:T(8,128)(2,1)S(1)}, u32[]{:S(2)}, u32[]{:S(2)}) %all-to-all-start.1) | async-done | bytes 3145760 | tf_op jit(solution)/shard_map/all_to_all | solution.py:218
  235.2 2.3 fusion.53
  239.7 2.3 collective-permute-start.16
  245.4 2.8 dynamic-slice_add_fusion
  248.2 2.9 %collective-permute-start.17 = (f32[128,1536]{1,0:T(8,128)}, f32[128,1536]{1,0:T(8,128)}, u32[]{:S(2)}, u32[]{:S(2)}) collective-permute-start(f32[128,1536]{1,0:T(8,128)} %dynamic-slice_add_fusion), channel_id=1, source_target_pairs={{0,2},{1,3},{2,0},{3,1},{4,6},{5,7},{6,4},{7,5},{8,10},{9,11},{10,... | collective-permute-start | bytes 2359304 | tf_op jit(solution)/shard_map/ppermute | solution.py:43
  254.4 14.4 %collective-permute-done.17 = f32[128,1536]{1,0:T(8,128)} collective-permute-done((f32[128,1536]{1,0:T(8,128)}, f32[128,1536]{1,0:T(8,128)}, u32[]{:S(2)}, u32[]{:S(2)}) %collective-permute-start.17) | collective-permute-done | bytes 786464 | tf_op jit(solution)/shard_map/ppermute | solution.py:43
  270.6 3.0 %collective-permute-start.18 = (bf16[128,1536]{1,0:T(8,128)(2,1)S(1)}, bf16[128,1536]{1,0:T(8,128)(2,1)S(1)}, u32[]{:S(2)}, u32[]{:S(2)}) collective-permute-start(bf16[128,1536]{1,0:T(8,128)(2,1)S(1)} %get-tuple-element.6), channel_id=1, source_target_pairs={{0,2},{1,3},{2,0},{3,1},{4,6},{5,7},{6,4},{7,5},{8,10},{9,11},{10,... | collective-permute-start | bytes 1179656 | tf_op jit(solution)/shard_map/ppermute | solution.py:43
  273.5 8.1 %collective-permute-done.18 = bf16[128,1536]{1,0:T(8,128)(2,1)S(1)} collective-permute-done((bf16[128,1536]{1,0:T(8,128)(2,1)S(1)}, bf16[128,1536]{1,0:T(8,128)(2,1)S(1)}, u32[]{:S(2)}, u32[]{:S(2)}) %collective-permute-start.18) | collective-permute-done | bytes 393248 | tf_op jit(solution)/shard_map/ppermute | solution.py:43
  (131 shorter events, 61.5 us)
Async XLA Ops:
  0.0 52.1 %copy-start = (bf16[1536,2,256]{2,1,0:T(2,128)(2,1)S(1)}, bf16[1536,2,256]{2,1,0:T(2,128)(2,1)}, u32[]{:S(2)}) copy-start(bf16[1536,2,256]{2,1,0:T(2,128)(2,1)} %param.18) | copy-start | bytes 4718596
  0.0 14.4 %copy-start.24 = (s32[64]{0:T(128)S(1)}, s32[64]{0:T(128)}, u32[]{:S(2)}) copy-start(s32[64]{0:T(128)} %param.22) | copy-start | bytes 772
  1.2 4.0 %collective-permute-start = (bf16[128,2,128]{2,0,1:T(8,128)(2,1)S(1)}, bf16[128,2,128]{2,0,1:T(8,128)(2,1)S(1)}, u32[]{:S(2)}, u32[]{:S(2)}) collective-permute-start(bf16[128,2,128]{2,0,1:T(8,128)(2,1)S(1)} %bitcast.146), channel_id=1, source_target_pairs={{0,16},{4,20},{8,24},{12,28},{16,0},{20,4},{24,8},{28,12},{32,48},... | collective-permute-start | bytes 196616 | tf_op jit(solution)/shard_map/ppermute | solution.py:77
  2.9 49.8 %collective-permute-start.10 = (bf16[384,1536]{1,0:T(8,128)(2,1)}, bf16[384,1536]{1,0:T(8,128)(2,1)}, u32[]{:S(2)}, u32[]{:S(2)}) collective-permute-start(bf16[384,1536]{1,0:T(8,128)(2,1)} %param.19), channel_id=1, source_target_pairs={{0,16},{1,19},{2,18},{3,17},{4,20},{5,23},{6,22},{7,21},{8,24},{9,... | collective-permute-start | bytes 3538952 | tf_op jit(solution)/shard_map/ppermute | solution.py:66
  5.8 8.6 %collective-permute-start.1 = (bf16[2,128,2,128]{3,1,2,0:T(8,128)(2,1)}, bf16[2,128,2,128]{3,1,2,0:T(8,128)(2,1)}, u32[]{:S(2)}, u32[]{:S(2)}) collective-permute-start(bf16[2,128,2,128]{3,1,2,0:T(8,128)(2,1)} %get-tuple-element.19), channel_id=1, source_target_pairs={{0,4},{4,8},{8,12},{12,0},{16,20},{20,24},{24,28},{28,16},{32,36},... | collective-permute-start | bytes 393224 | tf_op jit(solution)/shard_map/ppermute | solution.py:82
  7.1 7.4 %collective-permute-start.2 = (bf16[2,128,2,128]{3,1,2,0:T(8,128)(2,1)}, bf16[2,128,2,128]{3,1,2,0:T(8,128)(2,1)}, u32[]{:S(2)}, u32[]{:S(2)}) collective-permute-start(bf16[2,128,2,128]{3,1,2,0:T(8,128)(2,1)} %get-tuple-element.19), channel_id=1, source_target_pairs={{0,8},{4,12},{8,0},{12,4},{16,24},{20,28},{24,16},{28,20},{32,40},... | collective-permute-start | bytes 393224 | tf_op jit(solution)/shard_map/ppermute | solution.py:82
  7.9 7.4 %collective-permute-start.3 = (bf16[2,128,2,128]{3,1,2,0:T(8,128)(2,1)}, bf16[2,128,2,128]{3,1,2,0:T(8,128)(2,1)}, u32[]{:S(2)}, u32[]{:S(2)}) collective-permute-start(bf16[2,128,2,128]{3,1,2,0:T(8,128)(2,1)} %get-tuple-element.19), channel_id=1, source_target_pairs={{0,12},{4,0},{8,4},{12,8},{16,28},{20,16},{24,20},{28,24},{32,44},... | collective-permute-start | bytes 393224 | tf_op jit(solution)/shard_map/ppermute | solution.py:82
  11.3 12.9 %copy-start.25 = (s32[64]{0:T(128)S(1)}, s32[64]{0:T(128)}, u32[]{:S(2)}) copy-start(s32[64]{0:T(128)} %param.21) | copy-start | bytes 772
  11.3 51.5 %collective-permute-start.13 = (bf16[1,576,1536]{2,1,0:T(8,128)(2,1)S(1)}, bf16[1,576,1536]{2,1,0:T(8,128)(2,1)}, u32[]{:S(2)}, u32[]{:S(2)}) collective-permute-start(bf16[1,576,1536]{2,1,0:T(8,128)(2,1)S(1)} %maximum_bitcast_fusion), channel_id=1, source_target_pairs={{0,16},{1,19},{2,18},{3,17},{4,20},{5,23},{6,22},{7,21},{8,24},{9,... | collective-permute-start | bytes 5308424 | tf_op jit(solution)/shard_map/ppermute | solution.py:66
  14.4 7.4 %copy-start.4 = (bf16[512,1536]{1,0:T(8,128)(2,1)S(1)}, bf16[512,1536]{1,0:T(8,128)(2,1)}, u32[]{:S(2)}) copy-start(bf16[512,1536]{1,0:T(8,128)(2,1)} %param.15) | copy-start | bytes 4718596
  17.4 13.7 %collective-permute-start.5 = (bf16[4,2,128,2,128]{4,2,3,1,0:T(8,128)(2,1)}, bf16[4,2,128,2,128]{4,2,3,1,0:T(8,128)(2,1)}, u32[]{:S(2)}, u32[]{:S(2)}) collective-permute-start(bf16[4,2,128,2,128]{4,2,3,1,0:T(8,128)(2,1)} %get-tuple-element.15), channel_id=1, source_target_pairs={{0,64},{4,68},{8,72},{12,76},{16,80},{20,84},{24,88},{28,92},{32,9... | collective-permute-start | bytes 1572872 | tf_op jit(solution)/shard_map/ppermute | solution.py:85
  20.3 23.3 %collective-permute-start.6 = (bf16[4,2,128,2,128]{4,2,3,1,0:T(8,128)(2,1)}, bf16[4,2,128,2,128]{4,2,3,1,0:T(8,128)(2,1)}, u32[]{:S(2)}, u32[]{:S(2)}) collective-permute-start(bf16[4,2,128,2,128]{4,2,3,1,0:T(8,128)(2,1)} %get-tuple-element.15), channel_id=1, source_target_pairs={{0,96},{4,100},{8,104},{12,108},{16,112},{20,116},{24,120},{28,124... | collective-permute-start | bytes 1572872 | tf_op jit(solution)/shard_map/ppermute | solution.py:85
  21.1 23.2 %collective-permute-start.4 = (bf16[4,2,128,2,128]{4,2,3,1,0:T(8,128)(2,1)}, bf16[4,2,128,2,128]{4,2,3,1,0:T(8,128)(2,1)}, u32[]{:S(2)}, u32[]{:S(2)}) collective-permute-start(bf16[4,2,128,2,128]{4,2,3,1,0:T(8,128)(2,1)} %get-tuple-element.15), channel_id=1, source_target_pairs={{0,32},{4,36},{8,40},{12,44},{16,48},{20,52},{24,56},{28,60},{32,6... | collective-permute-start | bytes 1572872 | tf_op jit(solution)/shard_map/ppermute | solution.py:85
  22.2 26.1 %copy-start.22 = (f32[1536]{0:T(1024)S(1)}, f32[1536]{0:T(1024)}, u32[]{:S(2)}) copy-start(f32[1536]{0:T(1024)} %param.16) | copy-start | bytes 18436
  24.2 24.1 %copy-start.5 = (bf16[512,1536]{1,0:T(8,128)(2,1)S(1)}, bf16[512,1536]{1,0:T(8,128)(2,1)}, u32[]{:S(2)}) copy-start(bf16[512,1536]{1,0:T(8,128)(2,1)} %param.15) | copy-start | bytes 4718596
  24.3 24.1 %copy-start.21 = (bf16[1536,384]{1,0:T(8,128)(2,1)S(1)}, bf16[1536,384]{1,0:T(8,128)(2,1)}, u32[]{:S(2)}) copy-start(bf16[1536,384]{1,0:T(8,128)(2,1)} %param.17) | copy-start | bytes 3538948
  47.4 26.3 %collective-permute-start.7 = (bf16[32,128,2,128]{3,1,2,0:T(8,128)(2,1)}, bf16[32,128,2,128]{3,1,2,0:T(8,128)(2,1)}, u32[]{:S(2)}, u32[]{:S(2)}) collective-permute-start(bf16[32,128,2,128]{3,1,2,0:T(8,128)(2,1)} %bitcast.12), channel_id=1, source_target_pairs={{0,1},{1,0},{2,3},{3,2},{4,5},{5,4},{6,7},{7,6},{8,9},{9,8},{10,11... | collective-permute-start | bytes 6291464 | tf_op jit(solution)/shard_map/ppermute | solution.py:43
  52.7 15.7 %collective-permute-start.11 = (bf16[384,1536]{1,0:T(8,128)(2,1)}, bf16[384,1536]{1,0:T(8,128)(2,1)}, u32[]{:S(2)}, u32[]{:S(2)}) collective-permute-start(bf16[384,1536]{1,0:T(8,128)(2,1)} %collective-permute-done.10), channel_id=1, source_target_pairs={{0,18},{1,17},{2,16},{3,19},{4,22},{5,21},{6,20},{7,23},{8,26},{9,... | collective-permute-start | bytes 3538952 | tf_op jit(solution)/shard_map/ppermute | solution.py:67
  62.8 44.6 %collective-permute-start.14 = (bf16[1,576,1536]{2,1,0:T(8,128)(2,1)}, bf16[1,576,1536]{2,1,0:T(8,128)(2,1)}, u32[]{:S(2)}, u32[]{:S(2)}) collective-permute-start(bf16[1,576,1536]{2,1,0:T(8,128)(2,1)} %collective-permute-done.13), channel_id=1, source_target_pairs={{0,18},{1,17},{2,16},{3,19},{4,22},{5,21},{6,20},{7,23},{8,26},{9,... | collective-permute-start | bytes 5308424 | tf_op jit(solution)/shard_map/ppermute | solution.py:67
  71.6 41.2 %collective-permute-start.12 = (bf16[768,1536]{1,0:T(8,128)(2,1)}, bf16[768,1536]{1,0:T(8,128)(2,1)}, u32[]{:S(2)}, u32[]{:S(2)}) collective-permute-start(bf16[768,1536]{1,0:T(8,128)(2,1)} %pad_maximum_fusion.2), channel_id=1, source_target_pairs={{0,1},{1,0},{2,3},{3,2},{4,5},{5,4},{6,7},{7,6},{8,9},{9,8},{10,11... | collective-permute-start | bytes 7077896 | tf_op jit(solution)/shard_map/ppermute | solution.py:43
  93.2 12.3 %collective-permute-start.8 = (bf16[512,384]{0,1:T(8,128)(2,1)S(1)}, bf16[512,384]{0,1:T(8,128)(2,1)S(1)}, u32[]{:S(2)}, u32[]{:S(2)}) collective-permute-start(bf16[512,384]{0,1:T(8,128)(2,1)S(1)} %bitcast.138), channel_id=1, source_target_pairs={{0,2},{1,3},{2,0},{3,1},{4,6},{5,7},{6,4},{7,5},{8,10},{9,11},{10,... | collective-permute-start | bytes 1179656 | tf_op jit(solution)/shard_map/ppermute | solution.py:43
  106.4 6.4 %collective-permute-start.9 = (bf16[512,768]{0,1:T(8,128)(2,1)}, bf16[512,768]{0,1:T(8,128)(2,1)}, u32[]{:S(2)}, u32[]{:S(2)}) collective-permute-start(bf16[512,768]{0,1:T(8,128)(2,1)} %pad_maximum_fusion.6), channel_id=1, source_target_pairs={{0,1},{1,0},{2,3},{3,2},{4,5},{5,4},{6,7},{7,6},{8,9},{9,8},{10,11... | collective-permute-start | bytes 2359304 | tf_op jit(solution)/shard_map/ppermute | solution.py:43
  107.4 5.5 %copy-start.7 = (bf16[512,1536]{1,0:T(8,128)(2,1)S(1)}, bf16[512,1536]{1,0:T(8,128)(2,1)}, u32[]{:S(2)}) copy-start(bf16[512,1536]{1,0:T(8,128)(2,1)} %param.15) | copy-start | bytes 4718596
  107.4 5.5 %copy-start.12 = (bf16[384,1536]{1,0:T(8,128)(2,1)S(1)}, bf16[384,1536]{1,0:T(8,128)(2,1)}, u32[]{:S(2)}) copy-start(bf16[384,1536]{1,0:T(8,128)(2,1)} %param.19) | copy-start | bytes 3538948
  107.4 5.5 %copy-start.16 = (bf16[512,384]{0,1:T(8,128)(2,1)S(1)}, bf16[512,384]{0,1:T(8,128)(2,1)}, u32[]{:S(2)}) copy-start(bf16[512,384]{0,1:T(8,128)(2,1)} %copy-done.15) | copy-start | bytes 1179652
  111.2 17.4 %collective-permute-start.15 = (bf16[2,576,1536]{2,1,0:T(8,128)(2,1)}, bf16[2,576,1536]{2,1,0:T(8,128)(2,1)}, u32[]{:S(2)}, u32[]{:S(2)}) collective-permute-start(bf16[2,576,1536]{2,1,0:T(8,128)(2,1)} %pad_maximum_fusion.1), channel_id=1, source_target_pairs={{0,1},{1,0},{2,3},{3,2},{4,5},{5,4},{6,7},{7,6},{8,9},{9,8},{10,11... | collective-permute-start | bytes 10616840 | tf_op jit(solution)/shard_map/ppermute | solution.py:43
  121.8 49.0 %all-to-all-start = ((bf16[32,32,1536]{2,1,0:T(8,128)(2,1)}), bf16[32,32,1536]{2,1,0:T(8,128)(2,1)}, u32[]{:S(2)}, u32[]{:S(2)}) async-start(bf16[32,32,1536]{2,1,0:T(8,128)(2,1)} %bitcast.133), calls=%async_computation | async-start | bytes 6291456 | tf_op jit(solution)/shard_map/all_to_all | solution.py:211
  187.9 47.3 %all-to-all-start.1 = ((bf16[32,32,1536]{2,1,0:T(8,128)(2,1)}), bf16[32,32,1536]{2,1,0:T(8,128)(2,1)S(1)}, u32[]{:S(2)}, u32[]{:S(2)}) async-start(bf16[32,32,1536]{2,1,0:T(8,128)(2,1)} %bitcast.134), calls=%async_computation.1 | async-start | bytes 6291456 | tf_op jit(solution)/shard_map/all_to_all | solution.py:218
  239.7 5.7 %collective-permute-start.16 = (f32[256,1536]{1,0:T(8,128)}, f32[256,1536]{1,0:T(8,128)}, u32[]{:S(2)}, u32[]{:S(2)}) collective-permute-start(f32[256,1536]{1,0:T(8,128)} %convolution_add_fusion), channel_id=1, source_target_pairs={{0,1},{1,0},{2,3},{3,2},{4,5},{5,4},{6,7},{7,6},{8,9},{9,8},{10,11... | collective-permute-start | bytes 4718600 | tf_op jit(solution)/shard_map/ppermute | solution.py:43
  248.2 20.5 %collective-permute-start.17 = (f32[128,1536]{1,0:T(8,128)}, f32[128,1536]{1,0:T(8,128)}, u32[]{:S(2)}, u32[]{:S(2)}) collective-permute-start(f32[128,1536]{1,0:T(8,128)} %dynamic-slice_add_fusion), channel_id=1, source_target_pairs={{0,2},{1,3},{2,0},{3,1},{4,6},{5,7},{6,4},{7,5},{8,10},{9,11},{10,... | collective-permute-start | bytes 2359304 | tf_op jit(solution)/shard_map/ppermute | solution.py:43
  270.6 11.0 %collective-permute-start.18 = (bf16[128,1536]{1,0:T(8,128)(2,1)S(1)}, bf16[128,1536]{1,0:T(8,128)(2,1)S(1)}, u32[]{:S(2)}, u32[]{:S(2)}) collective-permute-start(bf16[128,1536]{1,0:T(8,128)(2,1)S(1)} %get-tuple-element.6), channel_id=1, source_target_pairs={{0,2},{1,3},{2,0},{3,1},{4,6},{5,7},{6,4},{7,5},{8,10},{9,11},{10,... | collective-permute-start | bytes 1179656 | tf_op jit(solution)/shard_map/ppermute | solution.py:43
  281.6 4.1 %collective-permute-start.19 = (bf16[256,1536]{1,0:T(8,128)(2,1)S(1)}, bf16[256,1536]{1,0:T(8,128)(2,1)S(1)}, u32[]{:S(2)}, u32[]{:S(2)}) collective-permute-start(bf16[256,1536]{1,0:T(8,128)(2,1)S(1)} %constant_dynamic-update-slice_fusion.2), channel_id=1, source_target_pairs={{0,1},{1,0},{2,3},{3,2},{4,5},{5,4},{6,7},{7,6},{8,9},{9,8},{10,11... | collective-permute-start | bytes 2359304 | tf_op jit(solution)/shard_map/ppermute | solution.py:43
  (16 other events, 40.6 us)

commit v4 on v2

--- a/solution.py
+++ b/solution.py
@@ -158,11 +158,9 @@
 
     prefix_a = prefix_of(pair_groups[0])
     prefix_b = prefix_of(pair_groups[1])
-    zero_q = jnp.zeros_like(query_rows)
     first3 = in_first[:, None, None]
-    query_ab = jnp.concatenate(
-        [jnp.where(first3, query_rows, zero_q), jnp.where(first3, zero_q, query_rows)], axis=-1
-    )
+    in_a = first3.astype(jnp.bfloat16)
+    query_ab = jnp.concatenate([query_rows * in_a, query_rows * (1 - in_a)], axis=-1)
     keys_ab = jnp.concatenate([prefix_a[:, 0], prefix_b[:, 0]], axis=-1)
     values_ab = jnp.concatenate([prefix_a[:, 1], prefix_b[:, 1]], axis=-1)
     pre_scores = jnp.einsum("thd,pd->htp", query_ab, keys_ab, preferred_element_type=jnp.float32)

time: 287 us -> 285 us (level)
  starting transfers between devices: 49 us -> 36.4 us
  waiting for transfers between devices: 133 us -> 145 us
    ppermute x9, starting transfers between devices: 17.5 us -> 10.5 us  [exp_flip(): return lax.ppermute(x, 'exp', [(e, e ^ bit) for e in range(n_exp)])]
    ppermute x9, waiting for transfers between devices: 36.9 us -> 42.3 us  [exp_flip(): return lax.ppermute(x, 'exp', [(e, e ^ bit) for e in range(n_exp)])]
    ppermute x3, waiting for transfers between devices: 0.33 us -> 5.77 us  [gather_prefix_halves(): lax.ppermute(along_z, 'req', req_shift_pairs(n_req, 'x', d))]
    ppermute x2, starting transfers between devices: 6.9 us -> 2.25 us  [far_relay(): hop = lax.ppermute(x, ('req', 'exp'), first)]
  transfers between devices with their start and end apart: 22 -> 22, of which waited for: 13 -> 13; matrix products, arithmetic and copies ran while one was open for 26% -> 25% of each run, Pallas kernels for 0% -> 0%
where the time goes in v4:
time: 285 us; the launch traced here: 284 us
  waiting for transfers between devices  145 us (51%)
  matrix products  49.8 us (17%)
  starting transfers between devices  36.4 us (13%)
  other arithmetic  29.4 us (10%)
  local copies, waits for them, and re-layouts  21.1 us (7%)
    ppermute x9, waiting for transfers between devices, exp_flip(): return lax.ppermute(x, 'exp', [(e, e ^ bit) for e in range(n_exp)])  42.3 us
    all_to_all x1, waiting for transfers between devices, body(): back = lax.all_to_all(part, 'req', split_axis=0, concat_axis=0, tiled=True)  39.6 us
    all_to_all x1, waiting for transfers between devices, body(): lax.all_to_all(send, 'req', split_axis=0, concat_axis=0, tiled=True)  36.2 us
    ppermute x3, waiting for transfers between devices, gather_prefix_halves(): lax.ppermute(along_x, 'req', req_shift_pairs(n_req, 'y', d))  18.1 us
    ppermute x9, starting transfers between devices, exp_flip(): return lax.ppermute(x, 'exp', [(e, e ^ bit) for e in range(n_exp)])  10.5 us
    dot_general x1, matrix products, body(): jnp.dot(hidden, down_full, preferred_element_type=jnp.float32)  10.2 us
    concatenate x2, other arithmetic, gather_exp_relay(): near = exp_flip(jnp.concatenate([x, far], axis=axis), n_exp, 1)  6.91 us
    dot_general x1, matrix products, body(): gate = jnp.dot(rows, gate_full, preferred_element_type=jnp.float32)  6.89 us
  transfers between devices with their start and end apart: 22, of which 13 were waited for; matrix products, arithmetic and copies ran while one was open for 25% of the time, Pallas kernels for 0%

profile of v4, /device:TPU:3, one launch (start us, length us, event | category | flops | bytes accessed | tf_op | source)
XLA Modules:
  0.0 284.1 jit_solution(5947877589481729745)
XLA Ops:
  2.9 2.2 collective-permute-start.10
  12.5 2.4 collective-permute-done.2
  19.2 2.6 collective-permute-start.5
  22.9 3.5 %fusion.35 = bf16[512,384]{0,1:T(8,128)(2,1)} fusion(bf16[1536,384]{1,0:T(8,128)(2,1)} %param.17, bf16[512,1536]{1,0:T(8,128)(2,1)} %param.15, f32[1536]{0:T(1024)S(1)} %copy-done.26, f32[512]{0:T(512)S(1)} %add_rsqrt_fusion.1), kind=kOutput, calls=%fused_computation.61 | convolution fusion | flops 607518720 | bytes 3153920 | tf_op jit(solution)/shard_map/dot_general | solution.py:136
  26.4 5.8 %collective-permute-done.4 = bf16[4,2,128,2,128]{4,2,3,1,0:T(8,128)(2,1)} collective-permute-done((bf16[4,2,128,2,128]{4,2,3,1,0:T(8,128)(2,1)}, bf16[4,2,128,2,128]{4,2,3,1,0:T(8,128)(2,1)}, u32[]{:S(2)}, u32[]{:S(2)}) %collective-permute-start.4) | collective-permute-done | bytes 524320 | tf_op jit(solution)/shard_map/ppermute | solution.py:85
  32.3 12.3 %collective-permute-done.5 = bf16[4,2,128,2,128]{4,2,3,1,0:T(8,128)(2,1)} collective-permute-done((bf16[4,2,128,2,128]{4,2,3,1,0:T(8,128)(2,1)}, bf16[4,2,128,2,128]{4,2,3,1,0:T(8,128)(2,1)}, u32[]{:S(2)}, u32[]{:S(2)}) %collective-permute-start.5) | collective-permute-done | bytes 524320 | tf_op jit(solution)/shard_map/ppermute | solution.py:85
  44.6 3.0 %pad_maximum_fusion.3 = bf16[4,4,2,128,2,128]{5,3,4,2,1,0:T(8,128)(2,1)} fusion(bf16[1,4,2,128,2,128]{5,3,4,2,1,0:T(8,128)(2,1)} %bitcast.16, bf16[1,4,2,128,2,128]{5,3,4,2,1,0:T(8,128)(2,1)} %bitcast.15, bf16[1,4,2,128,2,128]{5,3,4,2,1,0:T(8,128)(2,1)} %bitcast.14, bf16[1,4,2,128,2,128]{5,3,4,2,1,0:T(8,128)(2,1)S(1)} %copy-done.5), kind=kLoop, calls=%fused_computation.45 | loop fusion | flops 3145728 | bytes 4194304 | tf_op jit(solution)/shard_map/stack | solution.py:84
  58.0 2.3 fusion.19
  60.2 2.2 gather_fusion
  62.5 3.0 %gather_fusion.2 = bf16[8,128,2,128]{3,1,2,0:T(8,128)(2,1)} fusion(bf16[32,128,2,128]{3,1,2,0:T(8,128)(2,1)} %bitcast.17, s32[1024]{0:T(1024)S(1)} %get-tuple-element.36), kind=kCustom, calls=%fused_computation.2 | custom fusion | bytes 1048608 | tf_op jit(solution)/shard_map/gather | solution.py:154
  66.5 3.3 %collective-permute-done.11 = bf16[384,1536]{1,0:T(8,128)(2,1)} collective-permute-done((bf16[384,1536]{1,0:T(8,128)(2,1)}, bf16[384,1536]{1,0:T(8,128)(2,1)}, u32[]{:S(2)}, u32[]{:S(2)}) %collective-permute-start.11) | collective-permute-done | bytes 1179680 | tf_op jit(solution)/shard_map/ppermute | solution.py:67
  69.8 3.1 %pad_maximum_fusion.2 = bf16[768,1536]{1,0:T(8,128)(2,1)} fusion(bf16[384,1536]{1,0:T(8,128)(2,1)} %collective-permute-done.11, bf16[384,1536]{1,0:T(8,128)(2,1)} %param.19), kind=kLoop, calls=%fused_computation.44 | loop fusion | flops 4718592 | bytes 4718592 | tf_op jit(solution)/shard_map/concatenate | solution.py:72
  75.0 2.2 gather_fusion.1
  78.5 2.2 gather_fusion.3
  91.2 11.8 %collective-permute-done.8 = bf16[512,384]{0,1:T(8,128)(2,1)S(1)} collective-permute-done((bf16[512,384]{0,1:T(8,128)(2,1)S(1)}, bf16[512,384]{0,1:T(8,128)(2,1)S(1)}, u32[]{:S(2)}, u32[]{:S(2)}) %collective-permute-start.8) | collective-permute-done | bytes 393248 | tf_op jit(solution)/shard_map/ppermute | solution.py:43
  105.0 3.8 %pad_maximum_fusion.1 = bf16[2,576,1536]{2,1,0:T(8,128)(2,1)} fusion(bf16[1,576,1536]{2,1,0:T(8,128)(2,1)} %collective-permute-done.14, bf16[1,576,1536]{2,1,0:T(8,128)(2,1)S(1)} %bitcast.130), kind=kLoop, calls=%fused_computation.27 | loop fusion | flops 1769472 | bytes 7077888 | tf_op jit(solution)/shard_map/concatenate | solution.py:72
  110.5 5.1 %fusion.10 = (f32[512]{0:T(512)S(1)}, bf16[512,1536]{1,0:T(8,128)(2,1)S(1)}) fusion(bf16[768,1536]{1,0:T(8,128)(2,1)} %collective-permute-done.12, bf16[384,1536]{1,0:T(8,128)(2,1)} %collective-permute-done.11, bf16[384,1536]{1,0:T(8,128)(2,1)S(1)} %copy-done.13, bf16[512,768]{0,1:T(8,128)(2,1)} %collective-permute-done.9, ...), kind=kOutput, calls=%fused_computation.28 | convolution fusion | flops 2439511552 | bytes 9439232 | tf_op jit(solution)/shard_map/dot_general | solution.py:188
  115.7 3.8 %convolution_convert_fusion.1 = bf16[1024,1536]{1,0:T(8,128)(2,1)} fusion(pred[512,1024]{1,0:T(8,128)(4,1)S(1)} %fusion.2, bf16[512,1536]{1,0:T(8,128)(2,1)S(1)} %get-tuple-element.33, f32[1536]{0:T(1024)S(1)} %copy-done.27, f32[512]{0:T(512)S(1)} %add_rsqrt_fusion), kind=kOutput, calls=%fused_computation.26 | convolution fusion | flops 1615331328 | bytes 5251072 | tf_op jit(solution)/shard_map/tq,td->qd/dot_general | solution.py:207
  119.4 6.6 %all-to-all-start = ((bf16[32,32,1536]{2,1,0:T(8,128)(2,1)}), bf16[32,32,1536]{2,1,0:T(8,128)(2,1)}, u32[]{:S(2)}, u32[]{:S(2)}) async-start(bf16[32,32,1536]{2,1,0:T(8,128)(2,1)} %bitcast.134), calls=%async_computation | async-start | bytes 6291456 | tf_op jit(solution)/shard_map/all_to_all | solution.py:209
  126.0 3.4 %pad_maximum_fusion = bf16[4,576,1536]{2,1,0:T(8,128)(2,1)S(1)} fusion(bf16[2,576,1536]{2,1,0:T(8,128)(2,1)} %collective-permute-done.15, bf16[1,576,1536]{2,1,0:T(8,128)(2,1)} %collective-permute-done.14, bf16[1,576,1536]{2,1,0:T(8,128)(2,1)S(1)} %bitcast.131), kind=kLoop, calls=%fused_computation.12 | loop fusion | flops 7077888 | bytes 14155776 | tf_op jit(solution)/shard_map/concatenate | solution.py:73
  129.4 2.6 fusion.90
  132.1 36.2 %all-to-all-done = bf16[32,32,1536]{2,1,0:T(8,128)(2,1)} async-done(((bf16[32,32,1536]{2,1,0:T(8,128)(2,1)}), bf16[32,32,1536]{2,1,0:T(8,128)(2,1)}, u32[]{:S(2)}, u32[]{:S(2)}) %all-to-all-start) | async-done | bytes 3145760 | tf_op jit(solution)/shard_map/all_to_all | solution.py:209
  168.3 6.9 %fusion.92 = f32[1024,768]{1,0:T(8,128)} fusion(bf16[1024,1536]{1,0:T(8,128)(2,1)} %bitcast.40, bf16[768,1536]{1,0:T(8,128)(2,1)} %bitcast.138), kind=kOutput, calls=%fused_computation.200 | convolution fusion | flops 2415919104 | bytes 8650752 | tf_op jit(solution)/shard_map/dot_general | solution.py:211
  175.2 10.2 %convolution_convert_fusion = bf16[1024,1536]{1,0:T(8,128)(2,1)} fusion(bf16[768,1536]{1,0:T(8,128)(2,1)} %bitcast.137, f32[1024,768]{1,0:T(8,128)} %fusion.92, bf16[1024,1536]{1,0:T(8,128)(2,1)} %bitcast.40, bf16[768,1536]{1,0:T(8,128)(2,1)S(1)} %bitcast.136), kind=kOutput, calls=%fused_computation.25 | convolution fusion | flops 4835770368 | bytes 14155776 | tf_op jit(solution)/shard_map/dot_general | solution.py:214
  185.4 5.0 %all-to-all-start.1 = ((bf16[32,32,1536]{2,1,0:T(8,128)(2,1)}), bf16[32,32,1536]{2,1,0:T(8,128)(2,1)S(1)}, u32[]{:S(2)}, u32[]{:S(2)}) async-start(bf16[32,32,1536]{2,1,0:T(8,128)(2,1)} %bitcast.135), calls=%async_computation.1 | async-start | bytes 6291456 | tf_op jit(solution)/shard_map/all_to_all | solution.py:216
  190.4 2.7 select_reduce_fusion
  193.0 39.6 %all-to-all-done.1 = bf16[32,32,1536]{2,1,0:T(8,128)(2,1)S(1)} async-done(((bf16[32,32,1536]{2,1,0:T(8,128)(2,1)}), bf16[32,32,1536]{2,1,0:T(8,128)(2,1)S(1)}, u32[]{:S(2)}, u32[]{:S(2)}) %all-to-all-start.1) | async-done | bytes 3145760 | tf_op jit(solution)/shard_map/all_to_all | solution.py:216
  232.6 2.3 fusion.53
  237.1 2.3 collective-permute-start.16
  242.8 2.8 dynamic-slice_add_fusion
  249.6 16.7 %collective-permute-done.17 = f32[128,1536]{1,0:T(8,128)} collective-permute-done((f32[128,1536]{1,0:T(8,128)}, f32[128,1536]{1,0:T(8,128)}, u32[]{:S(2)}, u32[]{:S(2)}) %collective-permute-start.17) | collective-permute-done | bytes 786464 | tf_op jit(solution)/shard_map/ppermute | solution.py:43
  268.7 10.3 %collective-permute-done.18 = bf16[128,1536]{1,0:T(8,128)(2,1)S(1)} collective-permute-done((bf16[128,1536]{1,0:T(8,128)(2,1)S(1)}, bf16[128,1536]{1,0:T(8,128)(2,1)S(1)}, u32[]{:S(2)}, u32[]{:S(2)}) %collective-permute-start.18) | collective-permute-done | bytes 393248 | tf_op jit(solution)/shard_map/ppermute | solution.py:43
  (139 shorter events, 59.7 us)
Async XLA Ops:
  0.0 53.4 %copy-start = (bf16[1536,2,256]{2,1,0:T(2,128)(2,1)S(1)}, bf16[1536,2,256]{2,1,0:T(2,128)(2,1)}, u32[]{:S(2)}) copy-start(bf16[1536,2,256]{2,1,0:T(2,128)(2,1)} %param.18) | copy-start | bytes 4718596
  0.0 10.8 %copy-start.6 = (bf16[512,1536]{1,0:T(8,128)(2,1)S(1)}, bf16[512,1536]{1,0:T(8,128)(2,1)}, u32[]{:S(2)}) copy-start(bf16[512,1536]{1,0:T(8,128)(2,1)} %param.15) | copy-start | bytes 4718596
  1.2 5.5 %collective-permute-start = (bf16[128,2,128]{2,0,1:T(8,128)(2,1)S(1)}, bf16[128,2,128]{2,0,1:T(8,128)(2,1)S(1)}, u32[]{:S(2)}, u32[]{:S(2)}) collective-permute-start(bf16[128,2,128]{2,0,1:T(8,128)(2,1)S(1)} %bitcast.148), channel_id=1, source_target_pairs={{0,16},{4,20},{8,24},{12,28},{16,0},{20,4},{24,8},{28,12},{32,48},... | collective-permute-start | bytes 196616 | tf_op jit(solution)/shard_map/ppermute | solution.py:77
  2.9 51.1 %collective-permute-start.10 = (bf16[384,1536]{1,0:T(8,128)(2,1)}, bf16[384,1536]{1,0:T(8,128)(2,1)}, u32[]{:S(2)}, u32[]{:S(2)}) collective-permute-start(bf16[384,1536]{1,0:T(8,128)(2,1)} %param.19), channel_id=1, source_target_pairs={{0,16},{1,19},{2,18},{3,17},{4,20},{5,23},{6,22},{7,21},{8,24},{9,... | collective-permute-start | bytes 3538952 | tf_op jit(solution)/shard_map/ppermute | solution.py:66
  6.7 16.1 %copy-start.28 = (s32[64]{0:T(128)S(1)}, s32[64]{0:T(128)}, u32[]{:S(2)}) copy-start(s32[64]{0:T(128)} %param.22) | copy-start | bytes 772
  6.7 16.2 %copy-start.26 = (f32[1536]{0:T(1024)S(1)}, f32[1536]{0:T(1024)}, u32[]{:S(2)}) copy-start(f32[1536]{0:T(1024)} %param.16) | copy-start | bytes 18436
  6.8 5.7 %collective-permute-start.1 = (bf16[2,128,2,128]{3,1,2,0:T(8,128)(2,1)S(1)}, bf16[2,128,2,128]{3,1,2,0:T(8,128)(2,1)S(1)}, u32[]{:S(2)}, u32[]{:S(2)}) collective-permute-start(bf16[2,128,2,128]{3,1,2,0:T(8,128)(2,1)S(1)} %pad_maximum_fusion.9), channel_id=1, source_target_pairs={{0,4},{4,8},{8,12},{12,0},{16,20},{20,24},{24,28},{28,16},{32,36},... | collective-permute-start | bytes 393224 | tf_op jit(solution)/shard_map/ppermute | solution.py:82
  8.1 6.8 %collective-permute-start.2 = (bf16[2,128,2,128]{3,1,2,0:T(8,128)(2,1)S(1)}, bf16[2,128,2,128]{3,1,2,0:T(8,128)(2,1)S(1)}, u32[]{:S(2)}, u32[]{:S(2)}) collective-permute-start(bf16[2,128,2,128]{3,1,2,0:T(8,128)(2,1)S(1)} %pad_maximum_fusion.9), channel_id=1, source_target_pairs={{0,8},{4,12},{8,0},{12,4},{16,24},{20,28},{24,16},{28,20},{32,40},... | collective-permute-start | bytes 393224 | tf_op jit(solution)/shard_map/ppermute | solution.py:82
  8.9 8.0 %collective-permute-start.3 = (bf16[2,128,2,128]{3,1,2,0:T(8,128)(2,1)S(1)}, bf16[2,128,2,128]{3,1,2,0:T(8,128)(2,1)S(1)}, u32[]{:S(2)}, u32[]{:S(2)}) collective-permute-start(bf16[2,128,2,128]{3,1,2,0:T(8,128)(2,1)S(1)} %pad_maximum_fusion.9), channel_id=1, source_target_pairs={{0,12},{4,0},{8,4},{12,8},{16,28},{20,16},{24,20},{28,24},{32,44},... | collective-permute-start | bytes 393224 | tf_op jit(solution)/shard_map/ppermute | solution.py:82
  18.0 14.3 %collective-permute-start.4 = (bf16[4,2,128,2,128]{4,2,3,1,0:T(8,128)(2,1)}, bf16[4,2,128,2,128]{4,2,3,1,0:T(8,128)(2,1)}, u32[]{:S(2)}, u32[]{:S(2)}) collective-permute-start(bf16[4,2,128,2,128]{4,2,3,1,0:T(8,128)(2,1)} %get-tuple-element.19), channel_id=1, source_target_pairs={{0,32},{4,36},{8,40},{12,44},{16,48},{20,52},{24,56},{28,60},{32,6... | collective-permute-start | bytes 1572872 | tf_op jit(solution)/shard_map/ppermute | solution.py:85
  19.2 25.4 %collective-permute-start.5 = (bf16[4,2,128,2,128]{4,2,3,1,0:T(8,128)(2,1)}, bf16[4,2,128,2,128]{4,2,3,1,0:T(8,128)(2,1)}, u32[]{:S(2)}, u32[]{:S(2)}) collective-permute-start(bf16[4,2,128,2,128]{4,2,3,1,0:T(8,128)(2,1)} %get-tuple-element.19), channel_id=1, source_target_pairs={{0,64},{4,68},{8,72},{12,76},{16,80},{20,84},{24,88},{28,92},{32,9... | collective-permute-start | bytes 1572872 | tf_op jit(solution)/shard_map/ppermute | solution.py:85
  21.8 22.8 %collective-permute-start.6 = (bf16[4,2,128,2,128]{4,2,3,1,0:T(8,128)(2,1)}, bf16[4,2,128,2,128]{4,2,3,1,0:T(8,128)(2,1)}, u32[]{:S(2)}, u32[]{:S(2)}) collective-permute-start(bf16[4,2,128,2,128]{4,2,3,1,0:T(8,128)(2,1)} %get-tuple-element.19), channel_id=1, source_target_pairs={{0,96},{4,100},{8,104},{12,108},{16,112},{20,116},{24,120},{28,124... | collective-permute-start | bytes 1572872 | tf_op jit(solution)/shard_map/ppermute | solution.py:85
  22.9 21.6 %copy-start.5 = (bf16[1,4,2,128,2,128]{5,3,4,2,1,0:T(8,128)(2,1)S(1)}, bf16[1,4,2,128,2,128]{5,3,4,2,1,0:T(8,128)(2,1)}, u32[]{:S(2)}) copy-start(bf16[1,4,2,128,2,128]{5,3,4,2,1,0:T(8,128)(2,1)} %get-tuple-element.18) | copy-start | bytes 1572868
  26.4 24.8 %copy-start.29 = (s32[64]{0:T(128)S(1)}, s32[64]{0:T(128)}, u32[]{:S(2)}) copy-start(s32[64]{0:T(128)} %param.21) | copy-start | bytes 772
  26.4 39.0 %collective-permute-start.13 = (bf16[1,576,1536]{2,1,0:T(8,128)(2,1)S(1)}, bf16[1,576,1536]{2,1,0:T(8,128)(2,1)}, u32[]{:S(2)}, u32[]{:S(2)}) collective-permute-start(bf16[1,576,1536]{2,1,0:T(8,128)(2,1)S(1)} %bitcast.129), channel_id=1, source_target_pairs={{0,16},{1,19},{2,18},{3,17},{4,20},{5,23},{6,22},{7,21},{8,24},{9,... | collective-permute-start | bytes 5308424 | tf_op jit(solution)/shard_map/ppermute | solution.py:66
  44.6 8.7 %copy-start.25 = (s32[32]{0:T(128)S(1)}, s32[32]{0:T(128)}, u32[]{:S(2)}) copy-start(s32[32]{0:T(128)} %param.23) | copy-start | bytes 388
  47.5 27.5 %collective-permute-start.7 = (bf16[32,128,2,128]{3,1,2,0:T(8,128)(2,1)}, bf16[32,128,2,128]{3,1,2,0:T(8,128)(2,1)}, u32[]{:S(2)}, u32[]{:S(2)}) collective-permute-start(bf16[32,128,2,128]{3,1,2,0:T(8,128)(2,1)} %bitcast.17), channel_id=1, source_target_pairs={{0,1},{1,0},{2,3},{3,2},{4,5},{5,4},{6,7},{7,6},{8,9},{9,8},{10,11... | collective-permute-start | bytes 6291464 | tf_op jit(solution)/shard_map/ppermute | solution.py:43
  54.0 15.7 %collective-permute-start.11 = (bf16[384,1536]{1,0:T(8,128)(2,1)}, bf16[384,1536]{1,0:T(8,128)(2,1)}, u32[]{:S(2)}, u32[]{:S(2)}) collective-permute-start(bf16[384,1536]{1,0:T(8,128)(2,1)} %collective-permute-done.10), channel_id=1, source_target_pairs={{0,18},{1,17},{2,16},{3,19},{4,22},{5,21},{6,20},{7,23},{8,26},{9,... | collective-permute-start | bytes 3538952 | tf_op jit(solution)/shard_map/ppermute | solution.py:67
  65.5 39.6 %collective-permute-start.14 = (bf16[1,576,1536]{2,1,0:T(8,128)(2,1)}, bf16[1,576,1536]{2,1,0:T(8,128)(2,1)}, u32[]{:S(2)}, u32[]{:S(2)}) collective-permute-start(bf16[1,576,1536]{2,1,0:T(8,128)(2,1)} %collective-permute-done.13), channel_id=1, source_target_pairs={{0,18},{1,17},{2,16},{3,19},{4,22},{5,21},{6,20},{7,23},{8,26},{9,... | collective-permute-start | bytes 5308424 | tf_op jit(solution)/shard_map/ppermute | solution.py:67
  72.9 37.5 %collective-permute-start.12 = (bf16[768,1536]{1,0:T(8,128)(2,1)}, bf16[768,1536]{1,0:T(8,128)(2,1)}, u32[]{:S(2)}, u32[]{:S(2)}) collective-permute-start(bf16[768,1536]{1,0:T(8,128)(2,1)} %pad_maximum_fusion.2), channel_id=1, source_target_pairs={{0,1},{1,0},{2,3},{3,2},{4,5},{5,4},{6,7},{7,6},{8,9},{9,8},{10,11... | collective-permute-start | bytes 7077896 | tf_op jit(solution)/shard_map/ppermute | solution.py:43
  90.8 14.2 %copy-start.16 = (bf16[512,3,128]{0,2,1:T(8,128)(2,1)}, bf16[512,3,128]{0,2,1:T(8,128)(2,1)S(1)}, u32[]{:S(2)}) copy-start(bf16[512,3,128]{0,2,1:T(8,128)(2,1)S(1)} %fusion.36) | copy-start | bytes 1179652
  90.8 12.3 %collective-permute-start.8 = (bf16[512,384]{0,1:T(8,128)(2,1)S(1)}, bf16[512,384]{0,1:T(8,128)(2,1)S(1)}, u32[]{:S(2)}, u32[]{:S(2)}) collective-permute-start(bf16[512,384]{0,1:T(8,128)(2,1)S(1)} %bitcast.145), channel_id=1, source_target_pairs={{0,2},{1,3},{2,0},{3,1},{4,6},{5,7},{6,4},{7,5},{8,10},{9,11},{10,... | collective-permute-start | bytes 1179656 | tf_op jit(solution)/shard_map/ppermute | solution.py:43
  104.1 6.4 %collective-permute-start.9 = (bf16[512,768]{0,1:T(8,128)(2,1)}, bf16[512,768]{0,1:T(8,128)(2,1)}, u32[]{:S(2)}, u32[]{:S(2)}) collective-permute-start(bf16[512,768]{0,1:T(8,128)(2,1)} %pad_maximum_fusion.7), channel_id=1, source_target_pairs={{0,1},{1,0},{2,3},{3,2},{4,5},{5,4},{6,7},{7,6},{8,9},{9,8},{10,11... | collective-permute-start | bytes 2359304 | tf_op jit(solution)/shard_map/ppermute | solution.py:43
  105.0 5.5 %copy-start.8 = (bf16[512,1536]{1,0:T(8,128)(2,1)S(1)}, bf16[512,1536]{1,0:T(8,128)(2,1)}, u32[]{:S(2)}) copy-start(bf16[512,1536]{1,0:T(8,128)(2,1)} %param.15) | copy-start | bytes 4718596
  105.0 5.5 %copy-start.13 = (bf16[384,1536]{1,0:T(8,128)(2,1)S(1)}, bf16[384,1536]{1,0:T(8,128)(2,1)}, u32[]{:S(2)}) copy-start(bf16[384,1536]{1,0:T(8,128)(2,1)} %param.19) | copy-start | bytes 3538948
  108.8 17.2 %collective-permute-start.15 = (bf16[2,576,1536]{2,1,0:T(8,128)(2,1)}, bf16[2,576,1536]{2,1,0:T(8,128)(2,1)}, u32[]{:S(2)}, u32[]{:S(2)}) collective-permute-start(bf16[2,576,1536]{2,1,0:T(8,128)(2,1)} %pad_maximum_fusion.1), channel_id=1, source_target_pairs={{0,1},{1,0},{2,3},{3,2},{4,5},{5,4},{6,7},{7,6},{8,9},{9,8},{10,11... | collective-permute-start | bytes 10616840 | tf_op jit(solution)/shard_map/ppermute | solution.py:43
  119.4 48.9 %all-to-all-start = ((bf16[32,32,1536]{2,1,0:T(8,128)(2,1)}), bf16[32,32,1536]{2,1,0:T(8,128)(2,1)}, u32[]{:S(2)}, u32[]{:S(2)}) async-start(bf16[32,32,1536]{2,1,0:T(8,128)(2,1)} %bitcast.134), calls=%async_computation | async-start | bytes 6291456 | tf_op jit(solution)/shard_map/all_to_all | solution.py:209
  185.4 47.2 %all-to-all-start.1 = ((bf16[32,32,1536]{2,1,0:T(8,128)(2,1)}), bf16[32,32,1536]{2,1,0:T(8,128)(2,1)S(1)}, u32[]{:S(2)}, u32[]{:S(2)}) async-start(bf16[32,32,1536]{2,1,0:T(8,128)(2,1)} %bitcast.135), calls=%async_computation.1 | async-start | bytes 6291456 | tf_op jit(solution)/shard_map/all_to_all | solution.py:216
  237.1 5.7 %collective-permute-start.16 = (f32[256,1536]{1,0:T(8,128)}, f32[256,1536]{1,0:T(8,128)}, u32[]{:S(2)}, u32[]{:S(2)}) collective-permute-start(f32[256,1536]{1,0:T(8,128)} %convolution_add_fusion), channel_id=1, source_target_pairs={{0,1},{1,0},{2,3},{3,2},{4,5},{5,4},{6,7},{7,6},{8,9},{9,8},{10,11... | collective-permute-start | bytes 4718600 | tf_op jit(solution)/shard_map/ppermute | solution.py:43
  245.7 20.5 %collective-permute-start.17 = (f32[128,1536]{1,0:T(8,128)}, f32[128,1536]{1,0:T(8,128)}, u32[]{:S(2)}, u32[]{:S(2)}) collective-permute-start(f32[128,1536]{1,0:T(8,128)} %dynamic-slice_add_fusion), channel_id=1, source_target_pairs={{0,2},{1,3},{2,0},{3,1},{4,6},{5,7},{6,4},{7,5},{8,10},{9,11},{10,... | collective-permute-start | bytes 2359304 | tf_op jit(solution)/shard_map/ppermute | solution.py:43
  268.0 11.0 %collective-permute-start.18 = (bf16[128,1536]{1,0:T(8,128)(2,1)S(1)}, bf16[128,1536]{1,0:T(8,128)(2,1)S(1)}, u32[]{:S(2)}, u32[]{:S(2)}) collective-permute-start(bf16[128,1536]{1,0:T(8,128)(2,1)S(1)} %get-tuple-element.10), channel_id=1, source_target_pairs={{0,2},{1,3},{2,0},{3,1},{4,6},{5,7},{6,4},{7,5},{8,10},{9,11},{10,... | collective-permute-start | bytes 1179656 | tf_op jit(solution)/shard_map/ppermute | solution.py:43
  279.1 4.1 %collective-permute-start.19 = (bf16[256,1536]{1,0:T(8,128)(2,1)S(1)}, bf16[256,1536]{1,0:T(8,128)(2,1)S(1)}, u32[]{:S(2)}, u32[]{:S(2)}) collective-permute-start(bf16[256,1536]{1,0:T(8,128)(2,1)S(1)} %constant_dynamic-update-slice_fusion.2), channel_id=1, source_target_pairs={{0,1},{1,0},{2,3},{3,2},{4,5},{5,4},{6,7},{7,6},{8,9},{9,8},{10,11... | collective-permute-start | bytes 2359304 | tf_op jit(solution)/shard_map/ppermute | solution.py:43
  (20 other events, 55.5 us)
